TPU v7x, 256 devices: a whole 4x4x8 slice. The times are simulated.
256 devices in a mesh: chan: 8 (over z_hi, x), tm: 16 (over z_lo, y), dp: 2 (over core).
Axes of the slice: x: 4, y: 4, z: 8 (z_hi: 2, z_lo: 4; z = z_hi * 4 + z_lo), core: 2. Of those that a mesh axis runs over, the one named last changes fastest.
Arguments:
- contexts: bfloat16 [512, 4, 16384], P('tm', 'dp', 'chan'), may hold values from -6 to 6
- cotangent: bfloat16 [512, 4, 16384], P('tm', 'dp', 'chan'), may hold values from -6 to 6
- w_in: bfloat16 [16384, 8192], P('chan', 'tm'), may hold values from -0.046875 to 0.046875
- w_out: bfloat16 [8192, 16384], P('tm', 'chan'), may hold values from -0.0625 to 0.0625
- time_weight: bfloat16 [512, 512], replicated, may hold values from -0.25 to 0.25
Outputs:
- grad_contexts: bfloat16 [512, 4, 16384], P('tm', 'dp', 'chan')
- grad_w_in: float32 [16384, 8192], P('chan', ('tm', 'dp'))
- grad_w_out: float32 [8192, 16384], P(('tm', 'dp'), 'chan')
- grad_time: float32 [512, 512], replicated
All inputs are finite; a program needn't handle non-finite values.
Results may differ from a plain program's by a relative error of at most 0.0057.
Values may be sent and summed in bfloat16 or wider, within the bound.
No kernel may reach another device: no remote copies, remote signals or barrier semaphores. Data moves between devices by JAX's collectives and lax.ppermute only.
A program may use at most 192 MiB of HBM per device.

v0:
```python
import math

import jax
import jax.numpy as jnp
from jax import lax
from jax.sharding import PartitionSpec as P

tanh_scale = math.sqrt(2.0 / math.pi)
cubic_term = 0.044715


def gelu_pair(value):
    inner = jnp.tanh(tanh_scale * (value + cubic_term * value * value * value))
    result = 0.5 * value * (1.0 + inner)
    slope = 0.5 * (1.0 + inner) + 0.5 * value * (1.0 - inner * inner) * tanh_scale * (
        1.0 + 3.0 * cubic_term * value * value
    )
    return (result, slope)


def hidden_finish(hidden_pre, hidden_grad):
    act_hidden, slope_hidden = gelu_pair(hidden_pre)
    return (act_hidden.astype(jnp.bfloat16), (hidden_grad * slope_hidden).astype(jnp.bfloat16))


def on_device(contexts, cotangent, w_in, w_out, time_weight):
    local_len, batch_dev, width_dev = contexts.shape
    whole_x, whole_dy = (
        lax.all_gather(contexts, "tm", axis=0, tiled=True),
        lax.all_gather(cotangent, "tm", axis=0, tiled=True),
    )
    length = whole_x.shape[0]
    flat_x = whole_x.reshape(length, batch_dev * width_dev)
    pre_time = jnp.dot(time_weight, flat_x, preferred_element_type=jnp.float32)
    act_time, slope_time = gelu_pair(pre_time)
    mixed = (
        (flat_x.astype(jnp.float32) + act_time)
        .astype(jnp.bfloat16)
        .reshape(length * batch_dev, width_dev)
    )
    grad_rows = whole_dy.reshape(length * batch_dev, width_dev)
    hidden_part = jnp.dot(mixed, w_in, preferred_element_type=jnp.float32)
    hgrad_part = jnp.einsum("rc,hc->rh", grad_rows, w_out, preferred_element_type=jnp.float32)
    hidden_pre, hidden_grad = lax.psum((hidden_part, hgrad_part), "chan")
    activation, pre_grad = hidden_finish(hidden_pre, hidden_grad)
    win_part = jnp.einsum("rc,rh->ch", mixed, pre_grad, preferred_element_type=jnp.float32)
    wout_part = jnp.einsum("rh,rc->hc", activation, grad_rows, preferred_element_type=jnp.float32)
    grad_w_in, grad_w_out = (
        lax.psum_scatter(win_part, "dp", scatter_dimension=1, tiled=True),
        lax.psum_scatter(wout_part, "dp", scatter_dimension=0, tiled=True),
    )
    position = lax.axis_index("tm")
    my_rows = local_len * batch_dev
    feature_sum = lax.psum_scatter(
        jnp.einsum("rh,ch->rc", pre_grad, w_in, preferred_element_type=jnp.float32),
        "tm",
        scatter_dimension=0,
        tiled=True,
    )
    own_dy = cotangent.reshape(my_rows, width_dev)
    mixed_grad = (own_dy.astype(jnp.float32) + feature_sum).reshape(
        local_len, batch_dev * width_dev
    )
    own_slope = lax.dynamic_slice_in_dim(slope_time, position * local_len, local_len, 0)
    own_gate = (mixed_grad * own_slope).astype(jnp.bfloat16)
    all_gate = lax.all_gather(own_gate, "tm", axis=0, tiled=True)
    own_columns = lax.dynamic_slice_in_dim(time_weight, position * local_len, local_len, 1)
    back = jnp.einsum("tl,tk->lk", own_columns, all_gate, preferred_element_type=jnp.float32)
    grad_contexts = (
        (mixed_grad + back).reshape(local_len, batch_dev, width_dev).astype(jnp.bfloat16)
    )
    time_part = jnp.einsum("tk,lk->tl", own_gate, flat_x, preferred_element_type=jnp.float32)
    time_rows = lax.psum(time_part, ("chan", "dp"))
    grad_time = lax.all_gather(time_rows, "tm", axis=0, tiled=True)
    return (grad_contexts, grad_w_in, grad_w_out, grad_time)


def solution(mesh):
    return jax.shard_map(
        on_device,
        mesh=mesh,
        in_specs=(
            P("tm", "dp", "chan"),
            P("tm", "dp", "chan"),
            P("chan", "tm"),
            P("tm", "chan"),
            P(),
        ),
        out_specs=(P("tm", "dp", "chan"), P("chan", ("tm", "dp")), P(("tm", "dp"), "chan"), P()),
        check_vma=False,
    )
```

profile of v0, /device:TPU:1, one launch (start us, length us, event | category | flops | bytes accessed | tf_op | source)
XLA Modules:
  0.0 907.4 jit_solution(18198101720754820874)
XLA Ops:
  8.7 83.0 %all-gather.7.cloned.1.call-done = bf16[512,2,2048]{2,1,0:T(2,128)(2,1)} async-done(((bf16[32,2,2048]{2,1,0:T(2,128)(2,1)}), bf16[512,2,2048]{2,1,0:T(2,128)(2,1)}) %all-gather.7.cloned.1.call-update) | async-done | bytes 4194320 | tf_op jit(solution)/shard_map/all_gather | solution.py:29
  91.7 4.6 copy.9
  96.4 14.4 %fusion.1 = (f32[512,4096]{1,0:T(8,128)}, f32[512,4096]{1,0:T(8,128)}, bf16[512,4096]{1,0:T(8,128)(2,1)}, f32[512,4096]{1,0:T(8,128)}, f32[512,4096]{1,0:T(8,128)}) fusion(bf16[512,4096]{1,0:T(8,128)(2,1)S(1)} %bitcast.16, bf16[512,512]{1,0:T(8,128)(2,1)S(1)} %copy-done.9), kind=kOutput, calls=%fused_computation.2 | convolution fusion | flops 2170552320 | bytes 42467328 | tf_op jit(solution)/shard_map/dot_general | solution.py:34
  110.7 7.1 reshape.27
  117.9 61.4 %all-gather.5.cloned.1.call-done = bf16[512,2,2048]{2,1,0:T(2,128)(2,1)} async-done(((bf16[32,2,2048]{2,1,0:T(2,128)(2,1)}), bf16[512,2,2048]{2,1,0:T(2,128)(2,1)}) %all-gather.5.cloned.1.call-update) | async-done | bytes 4194320 | tf_op jit(solution)/shard_map/all_gather | solution.py:30
  179.3 7.2 reshape.25
  186.4 6.7 fusion.28
  193.1 3.7 fusion.29
  197.0 198.9 %all-reduce.6.cloned.1.call-done = (f32[1024,512]{1,0:T(8,128)}, f32[1024,512]{1,0:T(8,128)}) async-done(((f32[1024,512]{1,0:T(8,128)}, f32[1024,512]{1,0:T(8,128)}), (f32[1024,512]{1,0:T(8,128)}, f32[1024,512]{1,0:T(8,128)})) %all-reduce.6.cloned.1.call-update) | async-done | bytes 4194320 | tf_op jit(solution)/shard_map/psum | solution.py:44
  395.9 3.5 fusion.9
  400.4 5.6 fusion.30
  407.1 101.0 %reduce-scatter.4.cloned.1.call-done = f32[64,2048]{1,0:T(8,128)} async-done(((f32[1024,2048]{1,0:T(8,128)}), f32[64,2048]{1,0:T(8,128)}) %reduce-scatter.4.cloned.1.call-update) | async-done | bytes 524304 | tf_op jit(solution)/shard_map/reduce_scatter | solution.py:54
  509.3 1.7 fusion.19
  511.1 4.3 fusion.32
  515.4 170.7 %all-reduce.4.cloned.1.call-done = f32[32,512]{1,0:T(8,128)} async-done(((f32[32,512]{1,0:T(8,128)}), f32[32,512]{1,0:T(8,128)}) %all-reduce.4.cloned.1.call-update) | async-done | bytes 65552 | tf_op jit(solution)/shard_map/psum | solution.py:73
  686.9 6.5 fusion.31
  693.5 1.5 copy-done.5
  695.0 6.7 fusion.10
  701.8 56.8 %all-gather.11.cloned.1.call-done = f32[512,512]{1,0:T(8,128)} async-done(((f32[32,512]{1,0:T(8,128)}), f32[512,512]{1,0:T(8,128)}) %all-gather.11.cloned.1.call-update) | async-done | bytes 1048592 | tf_op jit(solution)/shard_map/all_gather | solution.py:74
  758.6 89.3 %all-gather.9.cloned.1.call-done = bf16[512,4096]{1,0:T(8,128)(2,1)} async-done(((bf16[32,4096]{1,0:T(8,128)(2,1)}), bf16[512,4096]{1,0:T(8,128)(2,1)}) %all-gather.9.cloned.1.call-update) | async-done | bytes 4194320 | tf_op jit(solution)/shard_map/all_gather | solution.py:66
  848.0 3.3 fusion.2
  852.1 24.6 %reduce-scatter.6.cloned.1.call-done = f32[2048,256]{1,0:T(8,128)} async-done(((f32[2048,512]{1,0:T(8,128)}), f32[2048,256]{1,0:T(8,128)}) %reduce-scatter.6.cloned.1.call-update) | async-done | bytes 2097168 | tf_op jit(solution)/shard_map/reduce_scatter | solution.py:49
  876.7 21.9 %reduce-scatter.8.cloned.1.call-done = f32[256,2048]{1,0:T(8,128)} async-done(((f32[512,2048]{1,0:T(8,128)}), f32[256,2048]{1,0:T(8,128)}) %reduce-scatter.8.cloned.1.call-update) | async-done | bytes 2097168 | tf_op jit(solution)/shard_map/reduce_scatter | solution.py:50
  898.6 2.3 copy.14
  (41 shorter events, 6.8 us)
Async XLA Ops:
  7.2 186.0 %copy-start = (bf16[2048,512]{1,0:T(8,128)(2,1)S(1)}, bf16[2048,512]{1,0:T(8,128)(2,1)}, u32[]{:S(2)}) copy-start(bf16[2048,512]{1,0:T(8,128)(2,1)} %param.7) | copy-start | bytes 6291460
  7.2 84.5 %all-gather.7.cloned.1.call-start = ((), (), s32[]{:S(2)}) async-start(), calls=%async_computation.4 | async-start | bytes 4456448 | tf_op jit(solution)/shard_map/all_gather | solution.py:29
  7.9 171.3 %all-gather.5.cloned.1.call-start = ((), (), s32[]{:S(2)}) async-start(), calls=%async_computation.3 | async-start | bytes 4456448 | tf_op jit(solution)/shard_map/all_gather | solution.py:30
  8.7 387.2 %all-reduce.6.cloned.1.call-start = ((), (), s32[]{:S(2)}) async-start(), calls=%async_computation.11 | async-start | bytes 8388608 | tf_op jit(solution)/shard_map/psum | solution.py:44
  91.7 4.7 copy-start.9
  96.4 14.4 %copy-start.2 = (bf16[64,8,2,2048]{3,1,2,0:T(8,128)(2,1)}, bf16[64,8,2,2048]{3,1,2,0:T(8,128)(2,1)S(1)}, u32[]{:S(2)}) copy-start(bf16[64,8,2,2048]{3,1,2,0:T(8,128)(2,1)S(1)} %copy.9) | copy-start | bytes 12582916
  186.4 6.7 copy-start.3
  196.8 311.2 %reduce-scatter.4.cloned.1.call-start = ((), (), s32[]{:S(2)}) async-start(), calls=%async_computation.5 | async-start | bytes 8912896 | tf_op jit(solution)/shard_map/reduce_scatter | solution.py:54
  399.5 1.0 copy-start.6
  406.0 0.9 copy-start.8
  406.1 280.1 %all-reduce.4.cloned.1.call-start = ((), (), s32[]{:S(2)}) async-start(), calls=%async_computation.9 | async-start | bytes 131072 | tf_op jit(solution)/shard_map/psum | solution.py:73
  511.0 4.3 copy-start.4
  511.1 175.9 %copy-start.7 = (bf16[1024,512]{1,0:T(8,128)(2,1)S(1)}, bf16[1024,512]{1,0:T(8,128)(2,1)}, u32[]{:S(2)}) copy-start(bf16[1024,512]{1,0:T(8,128)(2,1)} %copy-done.6) | copy-start | bytes 3145732
  515.4 243.2 %all-gather.11.cloned.1.call-start = ((), (), s32[]{:S(2)}) async-start(), calls=%async_computation.10 | async-start | bytes 1114112 | tf_op jit(solution)/shard_map/all_gather | solution.py:74
  686.1 161.8 %all-gather.9.cloned.1.call-start = ((), (), s32[]{:S(2)}) async-start(), calls=%async_computation.6 | async-start | bytes 4456448 | tf_op jit(solution)/shard_map/all_gather | solution.py:66
  686.9 189.9 %reduce-scatter.6.cloned.1.call-start = ((), (), s32[]{:S(2)}) async-start(), calls=%async_computation.7 | async-start | bytes 6291456 | tf_op jit(solution)/shard_map/reduce_scatter | solution.py:49
  693.5 1.6 copy-start.5
  693.5 205.2 %reduce-scatter.8.cloned.1.call-start = ((), (), s32[]{:S(2)}) async-start(), calls=%async_computation.8 | async-start | bytes 6291456 | tf_op jit(solution)/shard_map/reduce_scatter | solution.py:50
  848.0 52.9 %copy-start.1 = (bf16[2048,512]{1,0:T(8,128)(2,1)S(1)}, bf16[2048,512]{1,0:T(8,128)(2,1)}, u32[]{:S(2)}) copy-start(bf16[2048,512]{1,0:T(8,128)(2,1)} %param.7) | copy-start | bytes 6291460
Sparse Core Ops, SparseCore 0:
  9.8 81.8 all-gather.6
  93.5 85.7 all-gather.4
  196.9 198.9 all-reduce.5
  406.2 101.8 reduce-scatter.3
  515.5 170.5 all-reduce.3
  687.8 70.8 all-gather.10
  761.0 86.9 all-gather.8
  851.1 25.6 reduce-scatter.5
  879.9 18.7 reduce-scatter.7
where the time goes:
time: 908 us; the launch traced here: 907 us
  waiting for transfers between devices  810 us (89%)
  matrix products  51.1 us (6%)
  local copies, waits for them, and re-layouts  25.7 us (3%)
  between operations  13.9 us (2%)
    psum x1, waiting for transfers between devices, on_device(): hidden_pre, hidden_grad = lax.psum((hidden_part, hgrad_part), 'chan')  199 us
    psum x1, waiting for transfers between devices, on_device(): time_rows = lax.psum(time_part, ('chan', 'dp'))  171 us
    reduce_scatter x1, waiting for transfers between devices, on_device(): lax.psum_scatter(jnp.einsum('rh,ch->rc', pre_grad, w_in, preferred_elemen...  101 us
    all_gather x1, waiting for transfers between devices, on_device(): all_gate = lax.all_gather(own_gate, 'tm', axis=0, tiled=True)  89.3 us
    all_gather x1, waiting for transfers between devices, on_device(): lax.all_gather(contexts, 'tm', axis=0, tiled=True)  83 us
    all_gather x1, waiting for transfers between devices, on_device(): lax.all_gather(cotangent, 'tm', axis=0, tiled=True)  61.4 us
    all_gather x1, waiting for transfers between devices, on_device(): grad_time = lax.all_gather(time_rows, 'tm', axis=0, tiled=True)  56.8 us
    reduce_scatter x1, waiting for transfers between devices, on_device(): lax.psum_scatter(win_part, 'dp', scatter_dimension=1, tiled=True)  24.6 us
  transfers between devices with their start and end apart: 9, of which 9 were waited for; matrix products, arithmetic and copies ran while one was open for 5% of the time, Pallas kernels for 0%

commit v1 on v0

v1 whole, which is shorter than its diff:
```python
import math

import jax
import jax.numpy as jnp
from jax import lax
from jax.sharding import PartitionSpec as P

tanh_scale = math.sqrt(2.0 / math.pi)
cubic_term = 0.044715


def gelu_pair(value):
    inner = jnp.tanh(tanh_scale * (value + cubic_term * value * value * value))
    result = 0.5 * value * (1.0 + inner)
    slope = 0.5 * (1.0 + inner) + 0.5 * value * (1.0 - inner * inner) * tanh_scale * (
        1.0 + 3.0 * cubic_term * value * value
    )
    return (result, slope)


def hidden_finish(hidden_pre, hidden_grad):
    act_hidden, slope_hidden = gelu_pair(hidden_pre)
    return (act_hidden.astype(jnp.bfloat16), (hidden_grad * slope_hidden).astype(jnp.bfloat16))


def gather_a2a(x, axis_name, size, axis):
    b = jnp.broadcast_to(x[None], (size,) + x.shape)
    y = lax.all_to_all(b, axis_name, 0, 0, tiled=True)
    y = jnp.moveaxis(y, 0, axis)
    shape = list(x.shape)
    shape[axis] *= size
    return y.reshape(shape)


def scatter_a2a(p, axis_name, size):
    y = lax.all_to_all(p.reshape((size, p.shape[0] // size) + p.shape[1:]), axis_name, 0, 0, tiled=True)
    return y.sum(0)


def on_device(contexts, cotangent, w_in, w_out, time_weight, tm, chan, everyone, world):
    local_len, batch_dev, width_dev = contexts.shape
    pair = lax.all_gather(jnp.stack([contexts, cotangent]), "tm", axis=1, tiled=True)
    whole_x, whole_dy = pair[0], pair[1]
    length = whole_x.shape[0]
    flat_x = whole_x.reshape(length, batch_dev * width_dev)
    pre_time = jnp.dot(time_weight, flat_x, preferred_element_type=jnp.float32)
    act_time, slope_time = gelu_pair(pre_time)
    mixed = (
        (flat_x.astype(jnp.float32) + act_time)
        .astype(jnp.bfloat16)
        .reshape(length * batch_dev, width_dev)
    )
    grad_rows = whole_dy.reshape(length * batch_dev, width_dev)
    hidden_part = jnp.dot(mixed, w_in, preferred_element_type=jnp.float32)
    hgrad_part = jnp.einsum("rc,hc->rh", grad_rows, w_out, preferred_element_type=jnp.float32)
    hidden_pre, hidden_grad = scatter_a2a(jnp.stack([hidden_part, hgrad_part], 1), "chan", chan).swapaxes(0, 1)
    act_rows, grad_rows_h = hidden_finish(hidden_pre, hidden_grad)
    fin = gather_a2a(jnp.stack([act_rows, grad_rows_h], 1), "chan", chan, 0)
    activation, pre_grad = fin[:, 0], fin[:, 1]
    win_part = jnp.einsum("rc,rh->ch", mixed, pre_grad, preferred_element_type=jnp.float32)
    wout_part = jnp.einsum("rh,rc->hc", activation, grad_rows, preferred_element_type=jnp.float32)
    grad_w_in, grad_w_out = (
        lax.psum_scatter(win_part, "dp", scatter_dimension=1, tiled=True),
        lax.psum_scatter(wout_part, "dp", scatter_dimension=0, tiled=True),
    )
    share = jnp.einsum("rh,ch->rc", pre_grad, w_in, preferred_element_type=jnp.float32) + grad_rows.astype(
        jnp.float32
    ) * (1.0 / tm)
    share = share.reshape(length, batch_dev * width_dev)
    gate = share * slope_time
    gate_hi = gate.astype(jnp.bfloat16)
    gate_lo = (gate - gate_hi.astype(jnp.float32)).astype(jnp.bfloat16)
    gate = jnp.concatenate([gate_hi, gate_lo], axis=0)
    twice = jnp.concatenate([time_weight, time_weight], axis=0)
    back = jnp.einsum("tl,tk->lk", twice, gate, preferred_element_type=jnp.float32)
    grad_contexts = (
        lax.psum_scatter(share + back, "tm", scatter_dimension=0, tiled=True)
        .reshape(local_len, batch_dev, width_dev)
        .astype(jnp.bfloat16)
    )
    time_part = jnp.einsum("tk,lk->tl", gate_hi, flat_x, preferred_element_type=jnp.float32) + jnp.einsum(
        "tk,lk->tl", gate_lo, flat_x, preferred_element_type=jnp.float32
    )
    grad_time = gather_a2a(scatter_a2a(time_part, everyone, world), everyone, world, 0)
    return (grad_contexts, grad_w_in, grad_w_out, grad_time)


def solution(mesh):
    import functools

    step = functools.partial(
        on_device,
        tm=mesh.shape["tm"],
        chan=mesh.shape["chan"],
        everyone=("chan", "tm", "dp"),
        world=mesh.size,
    )
    return jax.shard_map(
        step,
        mesh=mesh,
        in_specs=(
            P("tm", "dp", "chan"),
            P("tm", "dp", "chan"),
            P("chan", "tm"),
            P("tm", "chan"),
            P(),
        ),
        out_specs=(P("tm", "dp", "chan"), P("chan", ("tm", "dp")), P(("tm", "dp"), "chan"), P()),
        check_vma=False,
    )
```

time: 908 us -> 545 us (0.60)
  waiting for transfers between devices: 810 us -> 130 us
  blocking collectives: 0 us -> 242 us
  local copies, waits for them, and re-layouts: 25.7 us -> 62.6 us
  starting transfers between devices: 0.54 us -> 14.3 us
  other arithmetic: 6.37 us -> 18.3 us
    psum x2 -> x0, waiting for transfers between devices: 370 us -> none  [the longest x1 199 us: on_device(): hidden_pre, hidden_grad = lax.psum((hidden_part, hgrad_part), 'chan')]
    all_to_all x0 -> x3, blocking collectives: none -> 242 us  [the longest x2 204 us: scatter_a2a(): lax.all_to_all(p.reshape((size, p.shape[0] // size) + p.shape[1:]), axis_...]
    all_gather x4 -> x1, waiting for transfers between devices: 291 us -> 106 us  [on_device(): lax.all_gather(jnp.stack([contexts, cotangent]), 'tm', axis=1, tiled=True)]
    reduce_scatter x1, waiting for transfers between devices: 101 us -> 0.01 us  [on_device(): lax.psum_scatter(share + back, 'tm', scatter_dimension=0, tiled=True)]
    reduce_scatter x1, waiting for transfers between devices: 24.6 us -> 0.01 us  [on_device(): lax.psum_scatter(win_part, 'dp', scatter_dimension=1, tiled=True)]
    all_to_all x0 -> x1, waiting for transfers between devices: none -> 19.8 us  [gather_a2a(): y = lax.all_to_all(b, axis_name, 0, 0, tiled=True)]
    reduce_scatter x1, waiting for transfers between devices: 21.9 us -> 3.42 us  [on_device(): lax.psum_scatter(wout_part, 'dp', scatter_dimension=0, tiled=True)]
    dot_general x0 -> x2, local copies, waits for them, and re-layouts: none -> 14.4 us  [the longest x1 7.25 us: on_device(): jnp.einsum('rc,hc->rh', grad_rows, w_out, preferred_element_type=jnp.floa...]
  transfers between devices with their start and end apart: 9 -> 5, of which waited for: 9 -> 3; matrix products, arithmetic and copies ran while one was open for 5% -> 8% of each run, Pallas kernels for 0% -> 0%
where the time goes in v1:
time: 545 us; the launch traced here: 537 us
  blocking collectives  242 us (44%)
  waiting for transfers between devices  130 us (24%)
  local copies, waits for them, and re-layouts  62.6 us (11%)
  matrix products  55.4 us (10%)
  other arithmetic  18.3 us (3%)
  starting transfers between devices  14.3 us (3%)
  between operations  14.1 us (3%)
    all_to_all x2, blocking collectives, scatter_a2a(): lax.all_to_all(p.reshape((size, p.shape[0] // size) + p.shape[1:]), axis_...  204 us
    all_gather x1, waiting for transfers between devices, on_device(): lax.all_gather(jnp.stack([contexts, cotangent]), 'tm', axis=1, tiled=True)  106 us
    all_to_all x1, blocking collectives, gather_a2a(): y = lax.all_to_all(b, axis_name, 0, 0, tiled=True)  38.3 us
    all_to_all x1, waiting for transfers between devices, gather_a2a(): y = lax.all_to_all(b, axis_name, 0, 0, tiled=True)  19.8 us
  transfers between devices with their start and end apart: 5, of which 3 were waited for; matrix products, arithmetic and copies ran while one was open for 8% of the time, Pallas kernels for 0%

profile of v1, /device:TPU:1, one launch (start us, length us, event | category | flops | bytes accessed | tf_op | source)
XLA Modules:
  0.0 536.7 jit_solution(5762201300547198620)
XLA Ops:
  7.2 2.7 pad_maximum_fusion.1
  10.0 106.4 %all-gather.2.cloned.1.call-done = bf16[2,512,2,2048]{3,2,1,0:T(2,128)(2,1)} async-done(((bf16[2,32,2,2048]{3,2,1,0:T(2,128)(2,1)}), bf16[2,512,2,2048]{3,2,1,0:T(2,128)(2,1)}) %all-gather.2.cloned.1.call-update) | async-done | bytes 8388624 | tf_op jit(solution)/shard_map/all_gather | solution.py:42
  116.4 7.9 %fusion.38 = (bf16[1,512,2,2048]{3,2,1,0:T(2,128)(2,1)S(1)}, bf16[1,512,2,2048]{3,2,1,0:T(2,128)(2,1)}) fusion(bf16[2,512,2,2048]{3,2,1,0:T(2,128)(2,1)} %all-gather.2.cloned.1.call-done), kind=kLoop, calls=%fused_computation.48 | loop fusion | bytes 16777216 | tf_op jit(solution)/shard_map/slice | solution.py:43
  124.4 4.4 copy.11
  128.7 7.3 %dot_general.42 = bf16[8,128,2048]{2,1,0:T(8,128)(2,1)} reshape(bf16[1,512,2,2048]{3,2,1,0:T(2,128)(2,1)} %get-tuple-element.7) | data formatting | bytes 8388608 | tf_op jit(solution)/shard_map/rc,hc->rh/dot_general | solution.py:55
  136.0 10.2 %add_convert_fusion = (bf16[512,4096]{1,0:T(8,128)(2,1)}, f32[4096,512]{0,1:T(8,128)}) fusion(bf16[512,4096]{1,0:T(8,128)(2,1)} %bitcast.76, bf16[512,512]{1,0:T(8,128)(2,1)S(1)} %copy-done.10), kind=kOutput, calls=%fused_computation.15 | convolution fusion | flops 2170552320 | bytes 17301504 | tf_op jit(solution)/shard_map/dot_general | solution.py:46
  146.2 7.1 %dot_general.39 = bf16[8,128,2048]{2,1,0:T(8,128)(2,1)} reshape(bf16[512,4096]{1,0:T(8,128)(2,1)} %get-tuple-element.10) | data formatting | bytes 8388608 | tf_op jit(solution)/shard_map/dot_general | solution.py:54
  153.3 5.4 fusion.20
  162.3 77.8 %all_to_all.20 = f32[8,128,2,512]{3,1,2,0:T(8,128)} all-to-all(f32[8,128,2,512]{3,1,2,0:T(8,128)S(1)} %copy.9), channel_id=1, replica_groups=mesh['chan'=8,'tm'=16,'dp'=2] {'chan'}, dimensions={0} | all-to-all | bytes 8388608 | tf_op jit(solution)/shard_map/all_to_all | solution.py:36
  244.5 4.4 all-to-all-start.1
  248.9 7.2 %reshape_squeeze.7 = bf16[1024,2048]{1,0:T(8,128)(2,1)} reshape(bf16[1,512,2,2048]{3,2,1,0:T(2,128)(2,1)} %get-tuple-element.7) | data formatting | bytes 8388608 | tf_op jit(solution)/shard_map/reshape;squeeze | solution.py:53
  256.1 19.8 %all-to-all-done.1 = bf16[8,128,2,512]{3,1,2,0:T(8,128)(2,1)} async-done(((bf16[8,128,2,512]{3,1,2,0:T(8,128)(2,1)}), bf16[8,128,2,512]{3,1,2,0:T(8,128)(2,1)}, u32[]{:S(2)}, u32[]{:S(2)}) %all-to-all-start.1) | async-done | bytes 2097184 | tf_op jit(solution)/shard_map/all_to_all | solution.py:28
  279.1 5.7 %multiply_add_fusion.1 = f32[1024,2048]{1,0:T(8,128)} fusion(bf16[1024,2048]{1,0:T(8,128)(2,1)S(1)} %copy-done.3, bf16[2048,512]{1,0:T(8,128)(2,1)S(1)} %copy-done, bf16[1024,2,512]{2,0,1:T(8,128)(2,1)S(1)} %bitcast.73), kind=kOutput, calls=%fused_computation.14 | convolution fusion | flops 2153775104 | bytes 15728640 | tf_op jit(solution)/shard_map/rh,ch->rc/dot_general | solution.py:66
  284.8 9.9 %reshape.177 = f32[512,4096]{1,0:T(8,128)} reshape(f32[1024,2048]{1,0:T(8,128)} %multiply_add_fusion.1) | data formatting | bytes 16777216 | tf_op jit(solution)/shard_map/reshape | solution.py:69
  294.7 10.6 %subtract_convert_fusion = (bf16[512,4096]{1,0:T(8,128)(2,1)S(1)}, bf16[512,4096]{1,0:T(8,128)(2,1)}) fusion(f32[512,4096]{1,0:T(8,128)} %reshape.177, f32[4096,512]{0,1:T(8,128)} %get-tuple-element.11), kind=kLoop, calls=%fused_computation.13 | loop fusion | flops 46137344 | bytes 25165824 | tf_op jit(solution)/shard_map/convert_element_type | solution.py:72
  307.3 10.5 %fusion.10 = f32[512,4096]{1,0:T(8,128)} fusion(f32[512,4096]{1,0:T(8,128)S(1)} %copy-done.2, bf16[512,4096]{1,0:T(8,128)(2,1)S(1)} %get-tuple-element.4, bf16[512,4096]{1,0:T(8,128)(2,1)} %get-tuple-element.5, bf16[512,512]{1,0:T(8,128)(2,1)S(1)} %copy-done.10), kind=kOutput, calls=%fused_computation.16 | convolution fusion | flops 4315938816 | bytes 25690112 | tf_op jit(solution)/shard_map/tl,tk->lk/dot_general | solution.py:75
  317.8 9.8 %reduce-scatter.6.cloned.1.call-start = ((), (), s32[]{:S(2)}) async-start(), calls=%async_computation.9 | async-start | bytes 6291456 | tf_op jit(solution)/shard_map/reduce_scatter | solution.py:63
  327.6 7.1 %reshape.178 = bf16[1024,2048]{1,0:T(8,128)(2,1)} reshape(bf16[512,4096]{1,0:T(8,128)(2,1)} %get-tuple-element.10) | data formatting | bytes 8388608 | tf_op jit(solution)/shard_map/reshape | solution.py:51
  334.7 6.5 %fusion.27 = f32[2048,512]{1,0:T(8,128)} fusion(bf16[1024,2048]{1,0:T(8,128)(2,1)} %reshape.178, bf16[1024,2,512]{2,0,1:T(8,128)(2,1)S(1)} %bitcast.74), kind=kOutput, calls=%fused_computation.31 | convolution fusion | flops 2147483648 | bytes 9437184 | tf_op jit(solution)/shard_map/rc,rh->ch/dot_general | solution.py:60
  341.3 6.5 %fusion.23 = f32[512,2048]{1,0:T(8,128)} fusion(bf16[1024,2048]{1,0:T(8,128)(2,1)} %reshape_squeeze.7, bf16[1024,2,512]{2,0,1:T(8,128)(2,1)S(1)} %bitcast.75), kind=kOutput, calls=%fused_computation.26 | convolution fusion | flops 2147483648 | bytes 9437184 | tf_op jit(solution)/shard_map/rh,rc->hc/dot_general | solution.py:61
  347.8 6.0 %fusion.39 = f32[512,512]{1,0:T(8,128)S(1)} fusion(bf16[512,4096]{1,0:T(8,128)(2,1)} %get-tuple-element.5, bf16[512,4096]{1,0:T(8,128)(2,1)} %bitcast.77), kind=kOutput, calls=%fused_computation.49 | convolution fusion | flops 2147483648 | bytes 9437184 | tf_op jit(solution)/shard_map/tk,lk->tl/dot_general | solution.py:81
  357.8 126.2 %all_to_all.21 = f32[256,2,512]{2,1,0:T(2,128)S(1)} all-to-all(f32[256,2,512]{2,1,0:T(2,128)} %reshape.179), channel_id=1, replica_groups=mesh['chan'=8,'tm'=16,'dp'=2] {'chan','tm','dp'}, dimensions={0} | all-to-all | bytes 2097152 | tf_op jit(solution)/shard_map/all_to_all | solution.py:36
  484.6 38.3 %all_to_all.22 = f32[256,2,512]{2,1,0:T(2,128)S(1)} all-to-all(f32[256,2,512]{2,1,0:T(2,128)S(1)} %broadcast_in_dim.5), channel_id=1, replica_groups=mesh['chan'=8,'tm'=16,'dp'=2] {'chan','tm','dp'}, dimensions={0} | all-to-all | bytes 2097152 | tf_op jit(solution)/shard_map/all_to_all | solution.py:28
  526.6 3.4 reduce-scatter.8.cloned.1.call-done
  (46 shorter events, 21.6 us)
Async XLA Ops:
  7.2 151.5 %copy-start = (bf16[2048,512]{1,0:T(8,128)(2,1)S(1)}, bf16[2048,512]{1,0:T(8,128)(2,1)}, u32[]{:S(2)}) copy-start(bf16[2048,512]{1,0:T(8,128)(2,1)} %param.7) | copy-start | bytes 6291460
  7.2 109.3 %all-gather.2.cloned.1.call-start = ((), (), s32[]{:S(2)}) async-start(), calls=%async_computation.7 | async-start | bytes 8912896 | tf_op jit(solution)/shard_map/all_gather | solution.py:42
  128.7 7.3 %copy-start.10 = (bf16[512,512]{1,0:T(8,128)(2,1)S(1)}, bf16[512,512]{1,0:T(8,128)(2,1)}, u32[]{:S(2)}) copy-start(bf16[512,512]{1,0:T(8,128)(2,1)} %param.9) | copy-start | bytes 1572868
  153.3 5.4 %copy-start.7 = (bf16[8,128,2048]{2,1,0:T(8,128)(2,1)S(1)}, bf16[8,128,2048]{2,1,0:T(8,128)(2,1)}, u32[]{:S(2)}) copy-start(bf16[8,128,2048]{2,1,0:T(8,128)(2,1)} %dot_general.39) | copy-start | bytes 12582916
  244.5 31.4 %all-to-all-start.1 = ((bf16[8,128,2,512]{3,1,2,0:T(8,128)(2,1)}), bf16[8,128,2,512]{3,1,2,0:T(8,128)(2,1)}, u32[]{:S(2)}, u32[]{:S(2)}) async-start(bf16[8,128,2,512]{3,1,2,0:T(8,128)(2,1)} %broadcast_in_dim.4), calls=%async_computation.1 | async-start | bytes 4194304 | tf_op jit(solution)/shard_map/all_to_all | solution.py:28
  248.9 275.7 %reduce-scatter.4.cloned.1.call-start = ((), (), s32[]{:S(2)}) async-start(), calls=%async_computation.8 | async-start | bytes 8912896 | tf_op jit(solution)/shard_map/reduce_scatter | solution.py:77
  275.9 3.2 copy-start.3
  277.8 1.3 copy-start.4
  294.7 12.6 %copy-start.2 = (f32[512,4096]{1,0:T(8,128)S(1)}, f32[512,4096]{1,0:T(8,128)}, u32[]{:S(2)}) copy-start(f32[512,4096]{1,0:T(8,128)} %reshape.177) | copy-start | bytes 25165828
  305.3 2.0 copy-start.8
  317.8 16.9 %copy-start.5 = (bf16[8,128,2,512]{3,1,0,2:T(8,128)(2,1)S(1)}, bf16[8,128,2,512]{3,1,0,2:T(8,128)(2,1)}, u32[]{:S(2)}) copy-start(bf16[8,128,2,512]{3,1,0,2:T(8,128)(2,1)} %copy-done.4) | copy-start | bytes 6291460
  317.8 208.8 %reduce-scatter.6.cloned.1.call-start = ((), (), s32[]{:S(2)}) async-start(), calls=%async_computation.9 | async-start | bytes 6291456 | tf_op jit(solution)/shard_map/reduce_scatter | solution.py:63
  341.2 188.8 %reduce-scatter.8.cloned.1.call-start = ((), (), s32[]{:S(2)}) async-start(), calls=%async_computation.10 | async-start | bytes 6291456 | tf_op jit(solution)/shard_map/reduce_scatter | solution.py:64
  347.8 6.0 %copy-start.6 = (bf16[64,8,2,2048]{3,1,2,0:T(8,128)(2,1)S(1)}, bf16[64,8,2,2048]{3,1,2,0:T(8,128)(2,1)}, u32[]{:S(2)}) copy-start(bf16[64,8,2,2048]{3,1,2,0:T(8,128)(2,1)} %copy.11) | copy-start | bytes 12582916
  347.8 6.0 %copy-start.9 = (bf16[512,4096]{1,0:T(8,128)(2,1)S(1)}, bf16[512,4096]{1,0:T(8,128)(2,1)}, u32[]{:S(2)}) copy-start(bf16[512,4096]{1,0:T(8,128)(2,1)} %copy-done.8) | copy-start | bytes 12582916
  357.8 172.2 %copy-start.1 = (bf16[2048,512]{1,0:T(8,128)(2,1)S(1)}, bf16[2048,512]{1,0:T(8,128)(2,1)}, u32[]{:S(2)}) copy-start(bf16[2048,512]{1,0:T(8,128)(2,1)} %param.7) | copy-start | bytes 6291460
Sparse Core Ops, SparseCore 0:
  10.4 106.0 all-gather.1
  317.9 166.7 reduce-scatter.3
  487.9 20.3 reduce-scatter.5
  511.2 18.7 reduce-scatter.7

commit v2 on v1

v2 whole, which is shorter than its diff:
```python
import functools
import math

import jax
import jax.numpy as jnp
from jax import lax
from jax.sharding import PartitionSpec as P

tanh_scale = math.sqrt(2.0 / math.pi)
cubic_term = 0.044715


def gelu_pair(value):
    inner = jnp.tanh(tanh_scale * (value + cubic_term * value * value * value))
    result = 0.5 * value * (1.0 + inner)
    slope = 0.5 * (1.0 + inner) + 0.5 * value * (1.0 - inner * inner) * tanh_scale * (
        1.0 + 3.0 * cubic_term * value * value
    )
    return (result, slope)


def hidden_finish(hidden_pre, hidden_grad):
    act_hidden, slope_hidden = gelu_pair(hidden_pre)
    return (act_hidden.astype(jnp.bfloat16), (hidden_grad * slope_hidden).astype(jnp.bfloat16))


def gather_a2a(x, axis_name, size):
    b = jnp.broadcast_to(x[None], (size,) + x.shape)
    y = lax.all_to_all(b, axis_name, 0, 0, tiled=True)
    return y.reshape((size * x.shape[0],) + x.shape[1:])


def scatter_a2a(p, axis_name, size):
    y = lax.all_to_all(p.reshape((size, p.shape[0] // size) + p.shape[1:]), axis_name, 0, 0, tiled=True)
    return y.sum(0)


def on_device(contexts, cotangent, w_in, w_out, time_weight, tm, chan, everyone, world):
    local_len, batch_dev, width_dev = contexts.shape
    own = jnp.stack([contexts, cotangent]).transpose(0, 2, 1, 3)
    pair = lax.all_gather(own, "tm", axis=2, tiled=True)
    whole_x, whole_dy = pair[0], pair[1]
    length = whole_x.shape[1]
    pre_time = jnp.einsum("tl,blc->btc", time_weight, whole_x, preferred_element_type=jnp.float32)
    act_time, slope_time = gelu_pair(pre_time)
    mixed = (whole_x.astype(jnp.float32) + act_time).astype(jnp.bfloat16)
    rows = batch_dev * length
    mixed_rows = mixed.reshape(rows, width_dev)
    grad_rows = whole_dy.reshape(rows, width_dev)
    hidden_part = jnp.dot(mixed_rows, w_in, preferred_element_type=jnp.float32)
    hgrad_part = jnp.einsum("rc,hc->rh", grad_rows, w_out, preferred_element_type=jnp.float32)
    summed = scatter_a2a(jnp.stack([hidden_part, hgrad_part], 1), "chan", chan)
    act_rows, pre_grad_rows = hidden_finish(summed[:, 0], summed[:, 1])
    fin = gather_a2a(jnp.stack([act_rows, pre_grad_rows], 1), "chan", chan)
    activation, pre_grad = fin[:, 0], fin[:, 1]
    win_part = jnp.einsum("rc,rh->ch", mixed_rows, pre_grad, preferred_element_type=jnp.float32)
    wout_part = jnp.einsum("rh,rc->hc", activation, grad_rows, preferred_element_type=jnp.float32)
    grad_w_in, grad_w_out = (
        lax.psum_scatter(win_part, "dp", scatter_dimension=1, tiled=True),
        lax.psum_scatter(wout_part, "dp", scatter_dimension=0, tiled=True),
    )
    share = jnp.einsum("rh,ch->rc", pre_grad, w_in, preferred_element_type=jnp.float32) + grad_rows.astype(
        jnp.float32
    ) * (1.0 / tm)
    share = share.reshape(batch_dev, length, width_dev)
    gate = (share * slope_time).astype(jnp.bfloat16)
    back = jnp.einsum("tl,btc->blc", time_weight, gate, preferred_element_type=jnp.float32)
    grad_own = lax.psum_scatter(share + back, "tm", scatter_dimension=1, tiled=True)
    grad_contexts = grad_own.astype(jnp.bfloat16).transpose(1, 0, 2)
    time_part = jnp.einsum("btc,blc->tl", gate, whole_x, preferred_element_type=jnp.float32)
    grad_time = gather_a2a(scatter_a2a(time_part, everyone, world), everyone, world)
    return (grad_contexts, grad_w_in, grad_w_out, grad_time)


def solution(mesh):
    step = functools.partial(
        on_device,
        tm=mesh.shape["tm"],
        chan=mesh.shape["chan"],
        everyone=("chan", "tm", "dp"),
        world=mesh.size,
    )
    return jax.shard_map(
        step,
        mesh=mesh,
        in_specs=(
            P("tm", "dp", "chan"),
            P("tm", "dp", "chan"),
            P("chan", "tm"),
            P("tm", "chan"),
            P(),
        ),
        out_specs=(P("tm", "dp", "chan"), P("chan", ("tm", "dp")), P(("tm", "dp"), "chan"), P()),
        check_vma=False,
    )
```

time: 545 us -> 478 us (0.88); the launches traced: 537 us -> 477 us
  local copies, waits for them, and re-layouts: 62.6 us -> 23.5 us
  blocking collectives: 242 us -> 278 us
  waiting for transfers between devices: 130 us -> 111 us
  matrix products: 55.4 us -> 39.3 us
  starting transfers between devices: 14.3 us -> 0.38 us
  other arithmetic: 18.3 us -> 11.1 us
    all_to_all x1 -> x2, blocking collectives: 38.3 us -> 86.6 us  [gather_a2a(): y = lax.all_to_all(b, axis_name, 0, 0, tiled=True)]
    all_to_all x1 -> x0, waiting for transfers between devices: 19.8 us -> none  [gather_a2a(): y = lax.all_to_all(b, axis_name, 0, 0, tiled=True)]
    reshape x4 -> x1, local copies, waits for them, and re-layouts: 20.3 us -> 1.69 us  [gather_a2a(): return y.reshape((size * x.shape[0],) + x.shape[1:])]
    all_to_all x2, blocking collectives: 204 us -> 192 us  [scatter_a2a(): lax.all_to_all(p.reshape((size, p.shape[0] // size) + p.shape[1:]), axis_...]
    dot_general x6 -> x5, matrix products: 37.8 us -> 28 us  [the longest x1 6.63 us: on_device(): jnp.einsum('tl,blc->btc', time_weight, whole_x, preferred_element_type=jn...]
    reduce_scatter x1, starting transfers between devices: 9.8 us -> 0.04 us  [on_device(): lax.psum_scatter(win_part, 'dp', scatter_dimension=1, tiled=True)]
    convert_element_type x2 -> x1, other arithmetic: 11.7 us -> 5.48 us  [on_device(): gate = (share * slope_time).astype(jnp.bfloat16)]
    dot_general x2, local copies, waits for them, and re-layouts: 14.4 us -> 8.45 us  [on_device(): jnp.einsum('btc,blc->tl', gate, whole_x, preferred_element_type=jnp.float32)]
  transfers between devices with their start and end apart: 5 -> 4, of which waited for: 3 -> 2; matrix products, arithmetic and copies ran while one was open for 8% -> 7% of each run, Pallas kernels for 0% -> 0%
where the time goes in v2:
time: 478 us; the launch traced here: 477 us
  blocking collectives  278 us (58%)
  waiting for transfers between devices  111 us (23%)
  matrix products  39.3 us (8%)
  local copies, waits for them, and re-layouts  23.5 us (5%)
  between operations  14 us (3%)
  other arithmetic  11.1 us (2%)
    all_to_all x2, blocking collectives, scatter_a2a(): lax.all_to_all(p.reshape((size, p.shape[0] // size) + p.shape[1:]), axis_...  192 us
    all_gather x1, waiting for transfers between devices, on_device(): pair = lax.all_gather(own, 'tm', axis=2, tiled=True)  107 us
    all_to_all x2, blocking collectives, gather_a2a(): y = lax.all_to_all(b, axis_name, 0, 0, tiled=True)  86.6 us
  transfers between devices with their start and end apart: 4, of which 2 were waited for; matrix products, arithmetic and copies ran while one was open for 7% of the time, Pallas kernels for 0%

profile of v2, /device:TPU:1, one launch (start us, length us, event | category | flops | bytes accessed | tf_op | source)
XLA Modules:
  0.0 477.1 jit_solution(14775185022718233797)
XLA Ops:
  7.2 1.3 copy_bitcast_fusion
  9.5 107.0 %all-gather.2.cloned.1.call-done = bf16[2,2,512,2048]{3,2,1,0:T(8,128)(2,1)} async-done(((bf16[2,2,32,2048]{3,2,1,0:T(8,128)(2,1)}), bf16[2,2,512,2048]{3,2,1,0:T(8,128)(2,1)}) %all-gather.2.cloned.1.call-update) | async-done | bytes 8388624 | tf_op jit(solution)/shard_map/all_gather | solution.py:41
  116.4 2.7 slice.25
  119.3 2.4 fusion.21
  121.7 1.7 slice-done.3
  123.5 6.6 %add_convert_fusion = (bf16[2,512,2048]{2,1,0:T(8,128)(2,1)S(1)}, f32[2,2048,512]{1,2,0:T(8,128)}) fusion(bf16[2,2,512,2048]{3,2,1,0:T(8,128)(2,1)S(1)} %bitcast.91, bf16[512,512]{1,0:T(8,128)(2,1)S(1)} %copy-done.7), kind=kOutput, calls=%fused_computation.12 | convolution fusion | flops 2170552320 | bytes 21495808 | tf_op jit(solution)/shard_map/tl,blc->btc/dot_general | solution.py:44
  130.1 2.3 fusion.18
  133.5 77.5 %all_to_all.20 = f32[8,128,2,512]{3,1,2,0:T(8,128)} all-to-all(f32[8,128,2,512]{3,1,2,0:T(8,128)S(1)} %copy.23), channel_id=1, replica_groups=mesh['chan'=8,'tm'=16,'dp'=2] {'chan'}, dimensions={0} | all-to-all | bytes 8388608 | tf_op jit(solution)/shard_map/all_to_all | solution.py:34
  211.0 2.7 reduce_sum.18
  214.1 34.7 %all_to_all.21 = bf16[8,128,2,512]{3,1,2,0:T(8,128)(2,1)S(1)} all-to-all(bf16[8,128,2,512]{3,1,2,0:T(8,128)(2,1)S(1)} %broadcast_in_dim.4), channel_id=1, replica_groups=mesh['chan'=8,'tm'=16,'dp'=2] {'chan'}, dimensions={0} | all-to-all | bytes 4194304 | tf_op jit(solution)/shard_map/all_to_all | solution.py:29
  249.0 2.4 multiply_add_fusion.1
  251.9 1.3 slice-done.1
  253.2 5.5 %fusion.6 = bf16[2,512,2048]{2,1,0:T(8,128)(2,1)S(1)} fusion(f32[2,512,2048]{2,1,0:T(8,128)S(1)} %bitcast.80, f32[2,2048,512]{1,2,0:T(8,128)S(1)} %bitcast.86), kind=kLoop, calls=%fused_computation.8 | loop fusion | flops 39845888 | bytes 20971520 | tf_op jit(solution)/shard_map/convert_element_type | solution.py:66
  258.7 1.9 copy-done.2
  260.6 6.0 %bitcast_add_fusion = f32[2,512,2048]{2,1,0:T(8,128)} fusion(f32[2,512,2048]{2,1,0:T(8,128)S(1)} %bitcast.81, bf16[2,512,2048]{2,1,0:T(8,128)(2,1)S(1)} %fusion.6, bf16[512,512]{1,0:T(8,128)(2,1)S(1)} %copy-done.7), kind=kOutput, calls=%fused_computation.9 | convolution fusion | flops 2149580800 | bytes 21495808 | tf_op jit(solution)/shard_map/tl,btc->blc/dot_general | solution.py:67
  266.7 1.5 copy-done.6
  268.2 6.6 %fusion.30 = f32[2048,512]{1,0:T(8,128)} fusion(bf16[1024,2048]{1,0:T(8,128)(2,1)} %bitcast.93, bf16[1024,2,512]{2,0,1:T(8,128)(2,1)S(1)} %bitcast.88), kind=kOutput, calls=%fused_computation.31 | convolution fusion | flops 2147483648 | bytes 9437184 | tf_op jit(solution)/shard_map/rc,rh->ch/dot_general | solution.py:56
  275.0 6.5 %fusion.29 = f32[512,2048]{1,0:T(8,128)} fusion(bf16[1024,2048]{1,0:T(8,128)(2,1)} %bitcast.83, bf16[1024,2,512]{2,0,1:T(8,128)(2,1)S(1)} %bitcast.89), kind=kOutput, calls=%fused_computation.29 | convolution fusion | flops 2147483648 | bytes 9437184 | tf_op jit(solution)/shard_map/rh,rc->hc/dot_general | solution.py:57
  281.6 7.6 %dot_general.48 = bf16[256,2,2,2048]{3,1,0,2:T(2,128)(2,1)} reshape(bf16[512,2,2048]{2,0,1:T(8,128)(2,1)} %bitcast.79) | data formatting | bytes 8388608 | tf_op jit(solution)/shard_map/btc,blc->tl/dot_general | solution.py:70
  289.2 6.5 %fusion.24 = f32[256,2,512]{2,0,1:T(8,128)S(1)} fusion(bf16[2,2,512,2048]{3,2,1,0:T(8,128)(2,1)} %all-gather.2.cloned.1.call-done, bf16[256,2,2,2048]{3,1,0,2:T(2,128)(2,1)} %dot_general.48), kind=kOutput, calls=%fused_computation.27 | convolution fusion | flops 2147483648 | bytes 9437184 | tf_op jit(solution)/shard_map/btc,blc->tl/dot_general | solution.py:70
  296.5 114.2 %all_to_all.22 = f32[256,2,512]{2,1,0:T(2,128)S(1)} all-to-all(f32[256,2,512]{2,1,0:T(2,128)S(1)} %copy.28), channel_id=1, replica_groups=mesh['chan'=8,'tm'=16,'dp'=2] {'chan','tm','dp'}, dimensions={0} | all-to-all | bytes 2097152 | tf_op jit(solution)/shard_map/all_to_all | solution.py:34
  411.3 51.9 %all_to_all.23 = f32[256,2,512]{2,1,0:T(2,128)S(1)} all-to-all(f32[256,2,512]{2,1,0:T(2,128)S(1)} %broadcast_in_dim.5), channel_id=1, replica_groups=mesh['chan'=8,'tm'=16,'dp'=2] {'chan','tm','dp'}, dimensions={0} | all-to-all | bytes 2097152 | tf_op jit(solution)/shard_map/all_to_all | solution.py:29
  463.2 1.7 reshape.44
  467.0 3.6 reduce-scatter.8.cloned.1.call-done
  (48 shorter events, 7.2 us)
Async XLA Ops:
  7.2 122.9 %copy-start = (bf16[2048,512]{1,0:T(8,128)(2,1)S(1)}, bf16[2048,512]{1,0:T(8,128)(2,1)}, u32[]{:S(2)}) copy-start(bf16[2048,512]{1,0:T(8,128)(2,1)} %param.7) | copy-start | bytes 6291460
  7.2 109.3 %all-gather.2.cloned.1.call-start = ((), (), s32[]{:S(2)}) async-start(), calls=%async_computation.7 | async-start | bytes 8912896 | tf_op jit(solution)/shard_map/all_gather | solution.py:41
  9.4 455.5 %reduce-scatter.4.cloned.1.call-start = ((), (), s32[]{:S(2)}) async-start(), calls=%async_computation.8 | async-start | bytes 8912896 | tf_op jit(solution)/shard_map/reduce_scatter | solution.py:68
  116.4 2.9 copy-start.8
  116.4 5.3 %slice-start.2 = ((s8[8388608]{0:T(1024)(128)(4,1)}), s8[4194304]{0:T(1024)(128)(4,1)S(1)}, s32[]{:S(2)}) async-start(s8[8388608]{0:T(1024)(128)(4,1)} %bitcast.90), calls=%async_computation.13 | async-start | bytes 8388608
  119.1 2.6 copy-start.3
  119.3 4.2 slice-start.3
  119.3 4.2 copy-start.7
  130.1 2.3 copy-start.9
  214.1 34.9 %copy-start.4 = (bf16[1,2,512,2048]{3,2,1,0:T(8,128)(2,1)S(1)}, bf16[1,2,512,2048]{3,2,1,0:T(8,128)(2,1)}, u32[]{:S(2)}) copy-start(bf16[1,2,512,2048]{3,2,1,0:T(8,128)(2,1)} %copy-done.3) | copy-start | bytes 12582916
  249.0 2.5 copy-start.5
  249.0 2.9 slice-start
  249.0 4.2 slice-start.1
  258.7 1.9 copy-start.2
  266.6 1.6 copy-start.6
  266.6 200.3 %reduce-scatter.6.cloned.1.call-start = ((), (), s32[]{:S(2)}) async-start(), calls=%async_computation.9 | async-start | bytes 6291456 | tf_op jit(solution)/shard_map/reduce_scatter | solution.py:59
  274.8 195.8 %reduce-scatter.8.cloned.1.call-start = ((), (), s32[]{:S(2)}) async-start(), calls=%async_computation.10 | async-start | bytes 6291456 | tf_op jit(solution)/shard_map/reduce_scatter | solution.py:60
  296.5 174.1 %copy-start.1 = (bf16[2048,512]{1,0:T(8,128)(2,1)S(1)}, bf16[2048,512]{1,0:T(8,128)(2,1)}, u32[]{:S(2)}) copy-start(bf16[2048,512]{1,0:T(8,128)(2,1)} %param.7) | copy-start | bytes 6291460
Sparse Core Ops, SparseCore 0:
  10.4 106.0 all-gather.1
  266.7 158.2 reduce-scatter.3
  428.2 20.6 reduce-scatter.5
  451.8 18.6 reduce-scatter.7

commit v3 on v2

--- a/solution.py
+++ b/solution.py
@@ -4,8 +4,11 @@
 import jax
 import jax.numpy as jnp
 from jax import lax
+from jax.sharding import Mesh
 from jax.sharding import PartitionSpec as P
 
+TM = ("tz", "ty")
+CHAN = ("zh", "cx")
 tanh_scale = math.sqrt(2.0 / math.pi)
 cubic_term = 0.044715
 
@@ -35,10 +38,10 @@
     return y.sum(0)
 
 
-def on_device(contexts, cotangent, w_in, w_out, time_weight, tm, chan, everyone, world):
+def on_device(contexts, cotangent, w_in, w_out, time_weight, tm, chan, chan_near, stages):
     local_len, batch_dev, width_dev = contexts.shape
     own = jnp.stack([contexts, cotangent]).transpose(0, 2, 1, 3)
-    pair = lax.all_gather(own, "tm", axis=2, tiled=True)
+    pair = lax.all_gather(own, TM, axis=2, tiled=True)
     whole_x, whole_dy = pair[0], pair[1]
     length = whole_x.shape[1]
     pre_time = jnp.einsum("tl,blc->btc", time_weight, whole_x, preferred_element_type=jnp.float32)
@@ -49,9 +52,11 @@
     grad_rows = whole_dy.reshape(rows, width_dev)
     hidden_part = jnp.dot(mixed_rows, w_in, preferred_element_type=jnp.float32)
     hgrad_part = jnp.einsum("rc,hc->rh", grad_rows, w_out, preferred_element_type=jnp.float32)
-    summed = scatter_a2a(jnp.stack([hidden_part, hgrad_part], 1), "chan", chan)
+    summed = scatter_a2a(jnp.stack([hidden_part, hgrad_part], 1), "cx", chan_near)
+    summed = scatter_a2a(summed, "zh", chan // chan_near)
     act_rows, pre_grad_rows = hidden_finish(summed[:, 0], summed[:, 1])
-    fin = gather_a2a(jnp.stack([act_rows, pre_grad_rows], 1), "chan", chan)
+    fin = gather_a2a(jnp.stack([act_rows, pre_grad_rows], 1), "zh", chan // chan_near)
+    fin = gather_a2a(fin, "cx", chan_near)
     activation, pre_grad = fin[:, 0], fin[:, 1]
     win_part = jnp.einsum("rc,rh->ch", mixed_rows, pre_grad, preferred_element_type=jnp.float32)
     wout_part = jnp.einsum("rh,rc->hc", activation, grad_rows, preferred_element_type=jnp.float32)
@@ -65,31 +70,35 @@
     share = share.reshape(batch_dev, length, width_dev)
     gate = (share * slope_time).astype(jnp.bfloat16)
     back = jnp.einsum("tl,btc->blc", time_weight, gate, preferred_element_type=jnp.float32)
-    grad_own = lax.psum_scatter(share + back, "tm", scatter_dimension=1, tiled=True)
+    grad_own = lax.psum_scatter(share + back, TM, scatter_dimension=1, tiled=True)
     grad_contexts = grad_own.astype(jnp.bfloat16).transpose(1, 0, 2)
     time_part = jnp.einsum("btc,blc->tl", gate, whole_x, preferred_element_type=jnp.float32)
-    grad_time = gather_a2a(scatter_a2a(time_part, everyone, world), everyone, world)
+    for names, size in stages:
+        time_part = scatter_a2a(time_part, names, size)
+    for names, size in stages[::-1]:
+        time_part = gather_a2a(time_part, names, size)
+    grad_time = time_part
     return (grad_contexts, grad_w_in, grad_w_out, grad_time)
 
 
 def solution(mesh):
+    chan, tm, dp = mesh.shape["chan"], mesh.shape["tm"], mesh.shape["dp"]
+    far, near_z = 2, 4
+    fine = Mesh(
+        mesh.devices.reshape(far, chan // far, near_z, tm // near_z, dp), ("zh", "cx", "tz", "ty", "dp")
+    )
     step = functools.partial(
         on_device,
-        tm=mesh.shape["tm"],
-        chan=mesh.shape["chan"],
-        everyone=("chan", "tm", "dp"),
-        world=mesh.size,
+        tm=tm,
+        chan=chan,
+        chan_near=chan // far,
+        stages=((("dp",), dp), (TM, tm), (CHAN, chan)),
     )
+    token = P(TM, "dp", CHAN)
     return jax.shard_map(
         step,
-        mesh=mesh,
-        in_specs=(
-            P("tm", "dp", "chan"),
-            P("tm", "dp", "chan"),
-            P("chan", "tm"),
-            P("tm", "chan"),
-            P(),
-        ),
-        out_specs=(P("tm", "dp", "chan"), P("chan", ("tm", "dp")), P(("tm", "dp"), "chan"), P()),
+        mesh=fine,
+        in_specs=(token, token, P(CHAN, TM), P(TM, CHAN), P()),
+        out_specs=(token, P(CHAN, TM + ("dp",)), P(TM + ("dp",), CHAN), P()),
         check_vma=False,
     )

time: 478 us -> 452 us (0.946)
  blocking collectives: 278 us -> 265 us
  local copies, waits for them, and re-layouts: 23.5 us -> 14.3 us
    all_to_all x2 -> x5, blocking collectives: 192 us -> 182 us  [scatter_a2a(): lax.all_to_all(p.reshape((size, p.shape[0] // size) + p.shape[1:]), axis_...]
    dot_general x2 -> x0, local copies, waits for them, and re-layouts: 8.45 us -> none  [on_device(): jnp.einsum('btc,blc->tl', gate, whole_x, preferred_element_type=jnp.float32)]
    all_to_all x2 -> x5, blocking collectives: 86.6 us -> 82.3 us  [gather_a2a(): y = lax.all_to_all(b, axis_name, 0, 0, tiled=True)]
  transfers between devices with their start and end apart: 4 -> 4, of which waited for: 2 -> 1; matrix products, arithmetic and copies ran while one was open for 7% -> 5% of each run, Pallas kernels for 0% -> 0%
where the time goes in v3:
time: 452 us
  blocking collectives  265 us (59%)
  waiting for transfers between devices  107 us (24%)
  matrix products  38.6 us (9%)
  local copies, waits for them, and re-layouts  14.3 us (3%)
  between operations  14 us (3%)
  other arithmetic  12.9 us (3%)
    all_to_all x5, blocking collectives, scatter_a2a(): lax.all_to_all(p.reshape((size, p.shape[0] // size) + p.shape[1:]), axis_...  182 us
    all_gather x1, waiting for transfers between devices, on_device(): pair = lax.all_gather(own, TM, axis=2, tiled=True)  107 us
    all_to_all x5, blocking collectives, gather_a2a(): y = lax.all_to_all(b, axis_name, 0, 0, tiled=True)  82.3 us
    unnamed x32, local copies, waits for them, and re-layouts  9.15 us
  transfers between devices with their start and end apart: 4, of which 1 were waited for; matrix products, arithmetic and copies ran while one was open for 5% of the time, Pallas kernels for 0%

profile of v3, /device:TPU:1, one launch (start us, length us, event | category | flops | bytes accessed | tf_op | source)
XLA Modules:
  0.0 451.7 jit_solution(17982651494056842236)
XLA Ops:
  9.5 107.0 %all-gather.2.cloned.1.call-done = bf16[2,2,512,2048]{3,2,1,0:T(8,128)(2,1)} async-done(((bf16[2,2,32,2048]{3,2,1,0:T(8,128)(2,1)}), bf16[2,2,512,2048]{3,2,1,0:T(8,128)(2,1)}) %all-gather.2.cloned.1.call-update) | async-done | bytes 8388624 | tf_op jit(solution)/shard_map/all_gather | solution.py:44
  116.4 2.7 slice.25
  119.3 2.4 fusion.20
  121.7 1.7 slice-done.3
  123.5 6.6 %add_convert_fusion = (bf16[2,512,2048]{2,1,0:T(8,128)(2,1)S(1)}, f32[2,2048,512]{1,2,0:T(8,128)}) fusion(bf16[2,2,512,2048]{3,2,1,0:T(8,128)(2,1)S(1)} %bitcast.102, bf16[512,512]{1,0:T(8,128)(2,1)S(1)} %copy-done.7), kind=kOutput, calls=%fused_computation.12 | convolution fusion | flops 2170552320 | bytes 21495808 | tf_op jit(solution)/shard_map/tl,blc->btc/dot_general | solution.py:47
  130.1 2.3 fusion.17
  133.3 51.6 %all_to_all.50 = f32[4,256,2,512]{3,1,2,0:T(8,128)} all-to-all(f32[4,256,2,512]{3,1,2,0:T(8,128)S(1)} %copy.61), channel_id=1, replica_groups=mesh['zh'=2,'cx'=4,'tz'=4,'ty'=4,'dp'=2] {'cx'}, dimensions={0} | all-to-all | bytes 8388608 | tf_op jit(solution)/shard_map/all_to_all | solution.py:37
  185.0 2.8 reduce_sum.45
  187.8 21.7 %all_to_all.51 = f32[2,128,2,512]{3,1,2,0:T(8,128)S(1)} all-to-all(f32[2,128,2,512]{3,1,2,0:T(8,128)S(1)} %copy.63), channel_id=1, replica_groups=mesh['zh'=2,'cx'=4,'tz'=4,'ty'=4,'dp'=2] {'zh'}, dimensions={0} | all-to-all | bytes 2097152 | tf_op jit(solution)/shard_map/all_to_all | solution.py:37
  211.7 11.7 %all_to_all.52 = bf16[2,128,2,512]{3,1,2,0:T(8,128)(2,1)S(1)} all-to-all(bf16[2,128,2,512]{3,1,2,0:T(8,128)(2,1)S(1)} %broadcast_in_dim.16), channel_id=1, replica_groups=mesh['zh'=2,'cx'=4,'tz'=4,'ty'=4,'dp'=2] {'zh'}, dimensions={0} | all-to-all | bytes 1048576 | tf_op jit(solution)/shard_map/all_to_all | solution.py:32
  223.7 18.1 %all_to_all.53 = bf16[4,256,2,512]{3,1,2,0:T(8,128)(2,1)S(1)} all-to-all(bf16[4,256,2,512]{3,1,2,0:T(8,128)(2,1)S(1)} %broadcast_in_dim.35), channel_id=1, replica_groups=mesh['zh'=2,'cx'=4,'tz'=4,'ty'=4,'dp'=2] {'cx'}, dimensions={0} | all-to-all | bytes 4194304 | tf_op jit(solution)/shard_map/all_to_all | solution.py:32
  242.0 2.4 multiply_add_fusion.1
  246.2 5.5 %fusion.6 = bf16[2,512,2048]{2,1,0:T(8,128)(2,1)S(1)} fusion(f32[2,512,2048]{2,1,0:T(8,128)S(1)} %bitcast.86, f32[2,2048,512]{1,2,0:T(8,128)S(1)} %bitcast.93), kind=kLoop, calls=%fused_computation.8 | loop fusion | flops 39845888 | bytes 20971520 | tf_op jit(solution)/shard_map/convert_element_type | solution.py:71
  251.6 1.9 copy-done.4
  253.6 6.0 %bitcast_add_fusion = f32[2,512,2048]{2,1,0:T(8,128)} fusion(f32[2,512,2048]{2,1,0:T(8,128)S(1)} %bitcast.87, bf16[2,512,2048]{2,1,0:T(8,128)(2,1)S(1)} %fusion.6, bf16[512,512]{1,0:T(8,128)(2,1)S(1)} %copy-done.8), kind=kOutput, calls=%fused_computation.9 | convolution fusion | flops 2149580800 | bytes 21495808 | tf_op jit(solution)/shard_map/tl,btc->blc/dot_general | solution.py:72
  261.1 6.5 %fusion.27 = f32[2048,512]{1,0:T(8,128)} fusion(bf16[1024,2048]{1,0:T(8,128)(2,1)} %bitcast.105, bf16[1024,2,512]{2,0,1:T(8,128)(2,1)S(1)} %bitcast.95), kind=kOutput, calls=%fused_computation.30 | convolution fusion | flops 2147483648 | bytes 9437184 | tf_op jit(solution)/shard_map/rc,rh->ch/dot_general | solution.py:61
  268.0 6.5 %fusion.26 = f32[512,2048]{1,0:T(8,128)} fusion(bf16[1024,2048]{1,0:T(8,128)(2,1)} %bitcast.89, bf16[1024,2,512]{2,0,1:T(8,128)(2,1)S(1)} %bitcast.96), kind=kOutput, calls=%fused_computation.28 | convolution fusion | flops 2147483648 | bytes 9437184 | tf_op jit(solution)/shard_map/rh,rc->hc/dot_general | solution.py:62
  274.5 5.8 %fusion.23 = f32[2,256,512]{2,1,0:T(8,128)S(1)} fusion(bf16[2,256,2,2048]{3,1,0,2:T(8,128)(2,1)} %bitcast.91, bf16[2,2,512,2048]{3,2,1,0:T(8,128)(2,1)} %all-gather.2.cloned.1.call-done), kind=kOutput, calls=%fused_computation.26 | convolution fusion | flops 2147483648 | bytes 9437184 | tf_op jit(solution)/shard_map/btc,blc->tl/dot_general | solution.py:75
  280.4 20.9 %all_to_all.54 = f32[2,256,512]{2,1,0:T(8,128)S(1)} all-to-all(f32[2,256,512]{2,1,0:T(8,128)S(1)} %fusion.23), channel_id=1, replica_groups=mesh['zh'=2,'cx'=4,'tz'=4,'ty'=4,'dp'=2] {'dp'}, dimensions={0} | all-to-all | bytes 2097152 | tf_op jit(solution)/shard_map/all_to_all | solution.py:37
  301.4 62.9 %all_to_all.55 = f32[16,16,512]{2,1,0:T(8,128)S(1)} all-to-all(f32[16,16,512]{2,1,0:T(8,128)S(1)} %bitcast.103), channel_id=1, replica_groups=mesh['zh'=2,'cx'=4,'tz'=4,'ty'=4,'dp'=2] {'tz','ty'}, dimensions={0} | all-to-all | bytes 1048576 | tf_op jit(solution)/shard_map/all_to_all | solution.py:37
  364.4 25.1 %all_to_all.56 = f32[8,2,512]{2,1,0:T(2,128)S(1)} all-to-all(f32[8,2,512]{2,1,0:T(2,128)S(1)} %reshape.58), channel_id=1, replica_groups=mesh['zh'=2,'cx'=4,'tz'=4,'ty'=4,'dp'=2] {'zh','cx'}, dimensions={0} | all-to-all | bytes 65536 | tf_op jit(solution)/shard_map/all_to_all | solution.py:37
  389.5 11.4 %all_to_all.57 = f32[8,2,512]{2,1,0:T(2,128)S(1)} all-to-all(f32[8,2,512]{2,1,0:T(2,128)S(1)} %broadcast_in_dim.36), channel_id=1, replica_groups=mesh['zh'=2,'cx'=4,'tz'=4,'ty'=4,'dp'=2] {'zh','cx'}, dimensions={0} | all-to-all | bytes 65536 | tf_op jit(solution)/shard_map/all_to_all | solution.py:32
  401.0 31.4 %all_to_all.58 = f32[16,16,512]{2,1,0:T(8,128)S(1)} all-to-all(f32[16,16,512]{2,1,0:T(8,128)S(1)} %broadcast_in_dim.38), channel_id=1, replica_groups=mesh['zh'=2,'cx'=4,'tz'=4,'ty'=4,'dp'=2] {'tz','ty'}, dimensions={0} | all-to-all | bytes 1048576 | tf_op jit(solution)/shard_map/all_to_all | solution.py:32
  432.6 9.6 %all_to_all.59 = f32[2,256,512]{2,1,0:T(8,128)S(1)} all-to-all(f32[2,256,512]{2,1,0:T(8,128)S(1)} %broadcast_in_dim.40), channel_id=1, replica_groups=mesh['zh'=2,'cx'=4,'tz'=4,'ty'=4,'dp'=2] {'dp'}, dimensions={0} | all-to-all | bytes 2097152 | tf_op jit(solution)/shard_map/all_to_all | solution.py:32
  (64 shorter events, 13.1 us)
Async XLA Ops:
  7.2 122.9 %copy-start = (bf16[2048,512]{1,0:T(8,128)(2,1)S(1)}, bf16[2048,512]{1,0:T(8,128)(2,1)}, u32[]{:S(2)}) copy-start(bf16[2048,512]{1,0:T(8,128)(2,1)} %param.7) | copy-start | bytes 6291460
  7.2 109.3 %all-gather.2.cloned.1.call-start = ((), (), s32[]{:S(2)}) async-start(), calls=%async_computation.13 | async-start | bytes 8912896 | tf_op jit(solution)/shard_map/all_gather | solution.py:44
  9.4 432.8 %reduce-scatter.4.cloned.1.call-start = ((), (), s32[]{:S(2)}) async-start(), calls=%async_computation.14 | async-start | bytes 8912896 | tf_op jit(solution)/shard_map/reduce_scatter | solution.py:73
  116.4 2.9 copy-start.9
  116.4 5.3 %slice-start.2 = ((s8[8388608]{0:T(1024)(128)(4,1)}), s8[4194304]{0:T(1024)(128)(4,1)S(1)}, s32[]{:S(2)}) async-start(s8[8388608]{0:T(1024)(128)(4,1)} %bitcast.101), calls=%async_computation.19 | async-start | bytes 8388608
  119.1 2.6 copy-start.2
  119.3 4.2 slice-start.3
  119.3 4.2 copy-start.7
  130.1 2.3 copy-start.10
  223.7 18.3 %copy-start.3 = (bf16[1,2,512,2048]{3,2,1,0:T(8,128)(2,1)S(1)}, bf16[1,2,512,2048]{3,2,1,0:T(8,128)(2,1)}, u32[]{:S(2)}) copy-start(bf16[1,2,512,2048]{3,2,1,0:T(8,128)(2,1)} %copy-done.2) | copy-start | bytes 12582916
  241.9 2.5 copy-start.5
  241.9 2.9 slice-start
  242.0 4.2 slice-start.1
  246.2 7.4 %copy-start.8 = (bf16[512,512]{1,0:T(8,128)(2,1)S(1)}, bf16[512,512]{1,0:T(8,128)(2,1)}, u32[]{:S(2)}) copy-start(bf16[512,512]{1,0:T(8,128)(2,1)} %param.9) | copy-start | bytes 1572868
  251.6 1.9 copy-start.4
  259.6 1.6 copy-start.6
  259.6 184.7 %reduce-scatter.6.cloned.1.call-start = ((), (), s32[]{:S(2)}) async-start(), calls=%async_computation.15 | async-start | bytes 6291456 | tf_op jit(solution)/shard_map/reduce_scatter | solution.py:64
  267.7 176.5 %reduce-scatter.8.cloned.1.call-start = ((), (), s32[]{:S(2)}) async-start(), calls=%async_computation.16 | async-start | bytes 6291456 | tf_op jit(solution)/shard_map/reduce_scatter | solution.py:65
  400.9 44.3 %copy-start.1 = (bf16[2048,512]{1,0:T(8,128)(2,1)S(1)}, bf16[2048,512]{1,0:T(8,128)(2,1)}, u32[]{:S(2)}) copy-start(bf16[2048,512]{1,0:T(8,128)(2,1)} %param.7) | copy-start | bytes 6291460
Sparse Core Ops, SparseCore 0:
  10.4 106.0 all-gather.1
  259.7 129.0 reduce-scatter.3
  391.9 20.7 reduce-scatter.5
  415.7 18.7 reduce-scatter.7

commit v4 on v3

--- a/solution.py
+++ b/solution.py
@@ -38,7 +38,7 @@
     return y.sum(0)
 
 
-def on_device(contexts, cotangent, w_in, w_out, time_weight, tm, chan, chan_near, stages):
+def on_device(contexts, cotangent, w_in, w_out, time_weight, tm, chan, chan_near, dp, stages):
     local_len, batch_dev, width_dev = contexts.shape
     own = jnp.stack([contexts, cotangent]).transpose(0, 2, 1, 3)
     pair = lax.all_gather(own, TM, axis=2, tiled=True)
@@ -58,12 +58,16 @@
     fin = gather_a2a(jnp.stack([act_rows, pre_grad_rows], 1), "zh", chan // chan_near)
     fin = gather_a2a(fin, "cx", chan_near)
     activation, pre_grad = fin[:, 0], fin[:, 1]
-    win_part = jnp.einsum("rc,rh->ch", mixed_rows, pre_grad, preferred_element_type=jnp.float32)
+    hidden_dev = pre_grad.shape[1]
+    win_part = jnp.einsum(
+        "rc,rkh->kch",
+        mixed_rows,
+        pre_grad.reshape(rows, dp, hidden_dev // dp),
+        preferred_element_type=jnp.float32,
+    )
     wout_part = jnp.einsum("rh,rc->hc", activation, grad_rows, preferred_element_type=jnp.float32)
-    grad_w_in, grad_w_out = (
-        lax.psum_scatter(win_part, "dp", scatter_dimension=1, tiled=True),
-        lax.psum_scatter(wout_part, "dp", scatter_dimension=0, tiled=True),
-    )
+    grad_w_in = scatter_a2a(win_part.reshape(dp * width_dev, hidden_dev // dp), "dp", dp)
+    grad_w_out = scatter_a2a(wout_part, "dp", dp)
     share = jnp.einsum("rh,ch->rc", pre_grad, w_in, preferred_element_type=jnp.float32) + grad_rows.astype(
         jnp.float32
     ) * (1.0 / tm)
@@ -92,7 +96,8 @@
         tm=tm,
         chan=chan,
         chan_near=chan // far,
-        stages=((("dp",), dp), (TM, tm), (CHAN, chan)),
+        dp=dp,
+        stages=(("dp", dp), ("cx", chan // far), ("zh", far), (TM, tm)),
     )
     token = P(TM, "dp", CHAN)
     return jax.shard_map(

time: 452 us -> 463 us (1.024)
  blocking collectives: 265 us -> 165 us
  starting transfers between devices: 0.38 us -> 73.2 us
  waiting for transfers between devices: 107 us -> 125 us
  other arithmetic: 12.9 us -> 21.3 us
  local copies, waits for them, and re-layouts: 14.3 us -> 22.6 us
    all_to_all x0 -> x5, starting transfers between devices: none -> 73.2 us  [the longest x3 42.9 us: scatter_a2a(): lax.all_to_all(p.reshape((size, p.shape[0] // size) + p.shape[1:]), axis_...]
    all_to_all x5, blocking collectives: 182 us -> 119 us  [scatter_a2a(): lax.all_to_all(p.reshape((size, p.shape[0] // size) + p.shape[1:]), axis_...]
    all_to_all x5 -> x4, blocking collectives: 82.3 us -> 46.1 us  [gather_a2a(): y = lax.all_to_all(b, axis_name, 0, 0, tiled=True)]
    all_to_all x0 -> x5, waiting for transfers between devices: none -> 17.5 us  [the longest x3 13.4 us: scatter_a2a(): lax.all_to_all(p.reshape((size, p.shape[0] // size) + p.shape[1:]), axis_...]
    reduce_sum x5 -> x8, other arithmetic: 3.85 us -> 12.2 us  [scatter_a2a(): return y.sum(0)]
  transfers between devices with their start and end apart: 4 -> 7, of which waited for: 1 -> 5; matrix products, arithmetic and copies ran while one was open for 5% -> 7% of each run, Pallas kernels for 0% -> 0%
where the time goes in v4:
time: 463 us; the launch traced here: 462 us
  blocking collectives  165 us (36%)
  waiting for transfers between devices  125 us (27%)
  starting transfers between devices  73.2 us (16%)
  matrix products  41.2 us (9%)
  local copies, waits for them, and re-layouts  22.6 us (5%)
  other arithmetic  21.3 us (5%)
  between operations  14.3 us (3%)
    all_to_all x5, blocking collectives, scatter_a2a(): lax.all_to_all(p.reshape((size, p.shape[0] // size) + p.shape[1:]), axis_...  119 us
    all_gather x1, waiting for transfers between devices, on_device(): pair = lax.all_gather(own, TM, axis=2, tiled=True)  107 us
    all_to_all x4, blocking collectives, gather_a2a(): y = lax.all_to_all(b, axis_name, 0, 0, tiled=True)  46.1 us
    all_to_all x3, starting transfers between devices, scatter_a2a(): lax.all_to_all(p.reshape((size, p.shape[0] // size) + p.shape[1:]), axis_...  42.9 us
    all_to_all x2, starting transfers between devices, gather_a2a(): y = lax.all_to_all(b, axis_name, 0, 0, tiled=True)  30.3 us
    all_to_all x3, waiting for transfers between devices, scatter_a2a(): lax.all_to_all(p.reshape((size, p.shape[0] // size) + p.shape[1:]), axis_...  13.4 us
    reduce_sum x8, other arithmetic, scatter_a2a(): return y.sum(0)  12.2 us
  transfers between devices with their start and end apart: 7, of which 5 were waited for; matrix products, arithmetic and copies ran while one was open for 7% of the time, Pallas kernels for 0%

profile of v4, /device:TPU:1, one launch (start us, length us, event | category | flops | bytes accessed | tf_op | source)
XLA Modules:
  0.0 462.2 jit_solution(10070382287601160127)
XLA Ops:
  9.5 107.0 %all-gather.2.cloned.1.call-done = bf16[2,2,512,2048]{3,2,1,0:T(8,128)(2,1)} async-done(((bf16[2,2,32,2048]{3,2,1,0:T(8,128)(2,1)}), bf16[2,2,512,2048]{3,2,1,0:T(8,128)(2,1)}) %all-gather.2.cloned.1.call-update) | async-done | bytes 8388624 | tf_op jit(solution)/shard_map/all_gather | solution.py:44
  123.5 6.7 %add_convert_fusion = (bf16[2,512,2048]{2,1,0:T(8,128)(2,1)S(1)}, f32[2,2048,512]{1,2,0:T(8,128)}) fusion(bf16[2,2,512,2048]{3,2,1,0:T(8,128)(2,1)S(1)} %bitcast.112, bf16[512,512]{1,0:T(8,128)(2,1)S(1)} %copy-done.5), kind=kOutput, calls=%fused_computation.12 | convolution fusion | flops 2170552320 | bytes 21495808 | tf_op jit(solution)/shard_map/tl,blc->btc/dot_general | solution.py:47
  133.4 51.6 %all_to_all.70 = f32[4,256,2,512]{3,1,2,0:T(8,128)} all-to-all(f32[4,256,2,512]{3,1,2,0:T(8,128)S(1)} %copy.72), channel_id=1, replica_groups=mesh['zh'=2,'cx'=4,'tz'=4,'ty'=4,'dp'=2] {'cx'}, dimensions={0} | all-to-all | bytes 8388608 | tf_op jit(solution)/shard_map/all_to_all | solution.py:37
  187.9 21.9 %all_to_all.71 = f32[2,128,2,512]{3,1,2,0:T(8,128)S(1)} all-to-all(f32[2,128,2,512]{3,1,2,0:T(8,128)S(1)} %copy.74), channel_id=1, replica_groups=mesh['zh'=2,'cx'=4,'tz'=4,'ty'=4,'dp'=2] {'zh'}, dimensions={0} | all-to-all | bytes 2097152 | tf_op jit(solution)/shard_map/all_to_all | solution.py:37
  212.1 11.7 %all_to_all.72 = bf16[2,128,2,512]{1,3,2,0:T(8,128)(2,1)S(1)} all-to-all(bf16[2,128,2,512]{1,3,2,0:T(8,128)(2,1)S(1)} %broadcast_in_dim.40), channel_id=1, replica_groups=mesh['zh'=2,'cx'=4,'tz'=4,'ty'=4,'dp'=2] {'zh'}, dimensions={0} | all-to-all | bytes 1048576 | tf_op jit(solution)/shard_map/all_to_all | solution.py:32
  224.5 18.6 %all_to_all.73 = bf16[4,256,2,512]{1,3,2,0:T(8,128)(2,1)} all-to-all(bf16[4,256,2,512]{1,3,2,0:T(8,128)(2,1)S(1)} %broadcast_in_dim.42), channel_id=1, replica_groups=mesh['zh'=2,'cx'=4,'tz'=4,'ty'=4,'dp'=2] {'cx'}, dimensions={0} | all-to-all | bytes 4194304 | tf_op jit(solution)/shard_map/all_to_all | solution.py:32
  247.2 5.0 %multiply_add_fusion.1 = f32[1024,2048]{1,0:T(8,128)S(1)} fusion(bf16[1,2,512,2048]{3,2,1,0:T(8,128)(2,1)} %copy-done.4, bf16[2048,512]{1,0:T(8,128)(2,1)S(1)} %copy-done, bf16[1024,2,512]{2,0,1:T(8,128)(2,1)} %bitcast.104), kind=kOutput, calls=%fused_computation.11 | convolution fusion | flops 2153775104 | bytes 15728640 | tf_op jit(solution)/shard_map/rh,ch->rc/dot_general | solution.py:71
  252.3 5.5 %fusion.6 = bf16[2,512,2048]{2,1,0:T(8,128)(2,1)S(1)} fusion(f32[2,512,2048]{2,1,0:T(8,128)S(1)} %bitcast.99, f32[2,2048,512]{1,2,0:T(8,128)S(1)} %bitcast.103), kind=kLoop, calls=%fused_computation.8 | loop fusion | flops 39845888 | bytes 20971520 | tf_op jit(solution)/shard_map/convert_element_type | solution.py:75
  259.8 6.0 %bitcast_add_fusion = f32[2,512,2048]{2,1,0:T(8,128)} fusion(f32[2,512,2048]{2,1,0:T(8,128)S(1)} %bitcast.100, bf16[2,512,2048]{2,1,0:T(8,128)(2,1)S(1)} %fusion.6, bf16[512,512]{1,0:T(8,128)(2,1)S(1)} %copy-done.6), kind=kOutput, calls=%fused_computation.9 | convolution fusion | flops 2149580800 | bytes 21495808 | tf_op jit(solution)/shard_map/tl,btc->blc/dot_general | solution.py:76
  265.8 5.8 %fusion.23 = f32[2,256,512]{2,1,0:T(8,128)S(1)} fusion(bf16[2,256,2,2048]{3,1,0,2:T(8,128)(2,1)} %bitcast.101, bf16[2,2,512,2048]{3,2,1,0:T(8,128)(2,1)} %all-gather.2.cloned.1.call-done), kind=kOutput, calls=%fused_computation.27 | convolution fusion | flops 2147483648 | bytes 9437184 | tf_op jit(solution)/shard_map/btc,blc->tl/dot_general | solution.py:79
  271.6 20.8 %all_to_all.74 = f32[2,256,512]{2,1,0:T(8,128)S(1)} all-to-all(f32[2,256,512]{2,1,0:T(8,128)S(1)} %fusion.23), channel_id=1, replica_groups=mesh['zh'=2,'cx'=4,'tz'=4,'ty'=4,'dp'=2] {'dp'}, dimensions={0} | all-to-all | bytes 2097152 | tf_op jit(solution)/shard_map/all_to_all | solution.py:37
  293.3 12.7 %all_to_all.75 = f32[4,64,512]{2,1,0:T(8,128)S(1)} all-to-all(f32[4,64,512]{2,1,0:T(8,128)} %bitcast.114), channel_id=1, replica_groups=mesh['zh'=2,'cx'=4,'tz'=4,'ty'=4,'dp'=2] {'cx'}, dimensions={0} | all-to-all | bytes 1048576 | tf_op jit(solution)/shard_map/all_to_all | solution.py:37
  312.7 6.2 %all-to-all-done.8 = f32[2,32,512]{2,1,0:T(8,128)S(1)} async-done(((f32[2,32,512]{2,1,0:T(8,128)}), f32[2,32,512]{2,1,0:T(8,128)S(1)}, u32[]{:S(2)}, u32[]{:S(2)}) %all-to-all-start.8) | async-done | bytes 131104 | tf_op jit(solution)/shard_map/all_to_all | solution.py:37
  319.6 28.9 %all-to-all-start.9 = ((f32[16,2,512]{2,1,0:T(2,128)}), f32[16,2,512]{2,1,0:T(2,128)S(1)}, u32[]{:S(2)}, u32[]{:S(2)}) async-start(f32[16,2,512]{2,1,0:T(2,128)} %reshape.65), calls=%async_computation.10 | async-start | bytes 131072 | tf_op jit(solution)/shard_map/all_to_all | solution.py:37
  348.5 6.5 %convolution_bitcast_fusion = f32[2,2048,256]{1,2,0:T(8,128)} fusion(bf16[1024,2,256]{0,2,1:T(8,128)(2,1)S(1)} %bitcast.115, bf16[1024,2048,1]{1,0,2:T(8,128)(2,1)} %bitcast.119), kind=kOutput, calls=%fused_computation.18 | convolution fusion | flops 2147483648 | bytes 9437184 | tf_op jit(solution)/shard_map/rc,rkh->kch/dot_general | solution.py:62
  359.3 18.5 %all-to-all-start.10 = ((f32[16,2,512]{2,1,0:T(2,128)}), f32[16,2,512]{2,1,0:T(2,128)S(1)}, u32[]{:S(2)}, u32[]{:S(2)}) async-start(f32[16,2,512]{2,1,0:T(2,128)} %broadcast_in_dim.43), calls=%async_computation.11 | async-start | bytes 131072 | tf_op jit(solution)/shard_map/all_to_all | solution.py:32
  377.9 6.5 %fusion.37 = f32[2,256,2048]{2,1,0:T(8,128)} fusion(bf16[2,256,1024]{2,1,0:T(8,128)(2,1)S(1)} %bitcast.116, bf16[1024,2048,1]{1,0,2:T(8,128)(2,1)} %bitcast.107), kind=kOutput, calls=%fused_computation.48 | convolution fusion | flops 2147483648 | bytes 9437184 | tf_op jit(solution)/shard_map/rh,rc->hc/dot_general | solution.py:68
  384.4 4.2 all-to-all-done.10
  388.6 10.7 %all-to-all-start.4 = ((f32[2,2048,256]{1,2,0:T(8,128)}), f32[2,2048,256]{1,2,0:T(8,128)}, u32[]{:S(2)}, u32[]{:S(2)}) async-start(f32[2,2048,256]{1,2,0:T(8,128)} %convolution_bitcast_fusion), calls=%async_computation.5 | async-start | bytes 8388608 | tf_op jit(solution)/shard_map/all_to_all | solution.py:37
  403.4 11.8 %all_to_all.76 = f32[2,256,2048]{2,1,0:T(8,128)} all-to-all(f32[2,256,2048]{2,1,0:T(8,128)} %fusion.37), channel_id=1, replica_groups=mesh['zh'=2,'cx'=4,'tz'=4,'ty'=4,'dp'=2] {'dp'}, dimensions={0} | all-to-all | bytes 8388608 | tf_op jit(solution)/shard_map/all_to_all | solution.py:37
  415.2 9.8 %all_to_all.77 = f32[2,32,512]{2,1,0:T(8,128)S(1)} all-to-all(f32[2,32,512]{2,1,0:T(8,128)S(1)} %broadcast_in_dim.45), channel_id=1, replica_groups=mesh['zh'=2,'cx'=4,'tz'=4,'ty'=4,'dp'=2] {'zh'}, dimensions={0} | all-to-all | bytes 262144 | tf_op jit(solution)/shard_map/all_to_all | solution.py:32
  425.9 11.7 %all-to-all-start.12 = ((f32[4,64,512]{2,1,0:T(8,128)}), f32[4,64,512]{2,1,0:T(8,128)S(1)}, u32[]{:S(2)}, u32[]{:S(2)}) async-start(f32[4,64,512]{2,1,0:T(8,128)} %broadcast_in_dim.47), calls=%async_computation.13 | async-start | bytes 1048576 | tf_op jit(solution)/shard_map/all_to_all | solution.py:32
  442.1 4.2 reduce_sum.75
  446.4 5.9 %all_to_all.78 = f32[2,256,512]{2,1,0:T(8,128)S(1)} all-to-all(f32[2,256,512]{2,1,0:T(8,128)S(1)} %broadcast_in_dim.49), channel_id=1, replica_groups=mesh['zh'=2,'cx'=4,'tz'=4,'ty'=4,'dp'=2] {'dp'}, dimensions={0} | all-to-all | bytes 2097152 | tf_op jit(solution)/shard_map/all_to_all | solution.py:32
  (73 shorter events, 49.6 us)
Async XLA Ops:
  7.2 123.0 %copy-start = (bf16[2048,512]{1,0:T(8,128)(2,1)S(1)}, bf16[2048,512]{1,0:T(8,128)(2,1)}, u32[]{:S(2)}) copy-start(bf16[2048,512]{1,0:T(8,128)(2,1)} %param.7) | copy-start | bytes 6291460
  7.2 109.3 %all-gather.2.cloned.1.call-start = ((), (), s32[]{:S(2)}) async-start(), calls=%async_computation.15 | async-start | bytes 8912896 | tf_op jit(solution)/shard_map/all_gather | solution.py:44
  9.4 442.9 %reduce-scatter.2.cloned.1.call-start = ((), (), s32[]{:S(2)}) async-start(), calls=%async_computation.16 | async-start | bytes 8912896 | tf_op jit(solution)/shard_map/reduce_scatter | solution.py:77
  116.4 2.9 copy-start.7
  116.4 5.3 %slice-start.2 = ((s8[8388608]{0:T(1024)(128)(4,1)}), s8[4194304]{0:T(1024)(128)(4,1)S(1)}, s32[]{:S(2)}) async-start(s8[8388608]{0:T(1024)(128)(4,1)} %bitcast.111), calls=%async_computation.19 | async-start | bytes 8388608
  119.1 2.6 copy-start.4
  119.3 4.2 slice-start.3
  119.3 4.2 copy-start.5
  130.1 2.3 copy-start.8
  247.2 5.0 %slice-start = ((s8[8388608]{0:T(1024)(128)(4,1)}), s8[4194304]{0:T(1024)(128)(4,1)S(1)}, s32[]{:S(2)}) async-start(s8[8388608]{0:T(1024)(128)(4,1)} %bitcast.102), calls=%async_computation.17 | async-start | bytes 8388608
  247.2 5.0 %slice-start.1 = ((s8[8388608]{0:T(1024)(128)(4,1)}), s8[4194304]{0:T(1024)(128)(4,1)S(1)}, s32[]{:S(2)}) async-start(s8[8388608]{0:T(1024)(128)(4,1)} %bitcast.102), calls=%async_computation.18 | async-start | bytes 8388608
  252.3 7.5 %copy-start.6 = (bf16[512,512]{1,0:T(8,128)(2,1)S(1)}, bf16[512,512]{1,0:T(8,128)(2,1)}, u32[]{:S(2)}) copy-start(bf16[512,512]{1,0:T(8,128)(2,1)} %param.9) | copy-start | bytes 1572868
  257.8 2.0 copy-start.2
  271.6 38.5 %copy-start.3 = (bf16[4,256,2,512]{3,1,0,2:T(8,128)(2,1)S(1)}, bf16[4,256,2,512]{3,1,0,2:T(8,128)(2,1)}, u32[]{:S(2)}) copy-start(bf16[4,256,2,512]{3,1,0,2:T(8,128)(2,1)} %copy.79) | copy-start | bytes 6291460
  306.7 12.2 %all-to-all-start.8 = ((f32[2,32,512]{2,1,0:T(8,128)}), f32[2,32,512]{2,1,0:T(8,128)S(1)}, u32[]{:S(2)}, u32[]{:S(2)}) async-start(f32[2,32,512]{2,1,0:T(8,128)} %bitcast.34), calls=%async_computation.9 | async-start | bytes 262144 | tf_op jit(solution)/shard_map/all_to_all | solution.py:37
  319.6 39.1 %all-to-all-start.9 = ((f32[16,2,512]{2,1,0:T(2,128)}), f32[16,2,512]{2,1,0:T(2,128)S(1)}, u32[]{:S(2)}, u32[]{:S(2)}) async-start(f32[16,2,512]{2,1,0:T(2,128)} %reshape.65), calls=%async_computation.10 | async-start | bytes 131072 | tf_op jit(solution)/shard_map/all_to_all | solution.py:37
  359.3 29.2 %all-to-all-start.10 = ((f32[16,2,512]{2,1,0:T(2,128)}), f32[16,2,512]{2,1,0:T(2,128)S(1)}, u32[]{:S(2)}, u32[]{:S(2)}) async-start(f32[16,2,512]{2,1,0:T(2,128)} %broadcast_in_dim.43), calls=%async_computation.11 | async-start | bytes 131072 | tf_op jit(solution)/shard_map/all_to_all | solution.py:32
  388.6 14.8 %all-to-all-start.4 = ((f32[2,2048,256]{1,2,0:T(8,128)}), f32[2,2048,256]{1,2,0:T(8,128)}, u32[]{:S(2)}, u32[]{:S(2)}) async-start(f32[2,2048,256]{1,2,0:T(8,128)} %convolution_bitcast_fusion), calls=%async_computation.5 | async-start | bytes 8388608 | tf_op jit(solution)/shard_map/all_to_all | solution.py:37
  425.9 20.4 %all-to-all-start.12 = ((f32[4,64,512]{2,1,0:T(8,128)}), f32[4,64,512]{2,1,0:T(8,128)S(1)}, u32[]{:S(2)}, u32[]{:S(2)}) async-start(f32[4,64,512]{2,1,0:T(8,128)} %broadcast_in_dim.47), calls=%async_computation.13 | async-start | bytes 1048576 | tf_op jit(solution)/shard_map/all_to_all | solution.py:32
  442.1 13.3 %copy-start.1 = (bf16[2048,512]{1,0:T(8,128)(2,1)S(1)}, bf16[2048,512]{1,0:T(8,128)(2,1)}, u32[]{:S(2)}) copy-start(bf16[2048,512]{1,0:T(8,128)(2,1)} %param.7) | copy-start | bytes 6291460
Sparse Core Ops, SparseCore 0:
  10.4 106.0 all-gather.1
  265.9 123.7 reduce-scatter.1

commit v5 on v3

--- a/solution.py
+++ b/solution.py
@@ -8,6 +8,7 @@
 from jax.sharding import PartitionSpec as P
 
 TM = ("tz", "ty")
+TM_SIZES = (4, 4)
 CHAN = ("zh", "cx")
 tanh_scale = math.sqrt(2.0 / math.pi)
 cubic_term = 0.044715
@@ -70,8 +71,11 @@
     share = share.reshape(batch_dev, length, width_dev)
     gate = (share * slope_time).astype(jnp.bfloat16)
     back = jnp.einsum("tl,btc->blc", time_weight, gate, preferred_element_type=jnp.float32)
-    grad_own = lax.psum_scatter(share + back, TM, scatter_dimension=1, tiled=True)
-    grad_contexts = grad_own.astype(jnp.bfloat16).transpose(1, 0, 2)
+    near_z = TM_SIZES[0]
+    grad_own = (share + back).reshape(batch_dev, near_z, tm // near_z, local_len, width_dev)
+    grad_own = lax.psum_scatter(grad_own, "ty", scatter_dimension=2, tiled=True)
+    grad_own = lax.psum_scatter(grad_own, "tz", scatter_dimension=1, tiled=True)
+    grad_contexts = grad_own.reshape(batch_dev, local_len, width_dev).astype(jnp.bfloat16).transpose(1, 0, 2)
     time_part = jnp.einsum("btc,blc->tl", gate, whole_x, preferred_element_type=jnp.float32)
     for names, size in stages:
         time_part = scatter_a2a(time_part, names, size)
@@ -83,7 +87,7 @@
 
 def solution(mesh):
     chan, tm, dp = mesh.shape["chan"], mesh.shape["tm"], mesh.shape["dp"]
-    far, near_z = 2, 4
+    far, near_z = 2, TM_SIZES[0]
     fine = Mesh(
         mesh.devices.reshape(far, chan // far, near_z, tm // near_z, dp), ("zh", "cx", "tz", "ty", "dp")
     )

time: 452 us -> 486 us (1.075)
  waiting for transfers between devices: 107 us -> 209 us
  blocking collectives: 265 us -> 195 us
    reduce_scatter x1 -> x2, waiting for transfers between devices: 0.01 us -> 102 us  [the longest x1 102 us: on_device(): grad_own = lax.psum_scatter(grad_own, 'ty', scatter_dimension=2, tiled=True)]
    all_to_all x5, blocking collectives: 182 us -> 123 us  [scatter_a2a(): lax.all_to_all(p.reshape((size, p.shape[0] // size) + p.shape[1:]), axis_...]
    all_to_all x5, blocking collectives: 82.3 us -> 72.1 us  [gather_a2a(): y = lax.all_to_all(b, axis_name, 0, 0, tiled=True)]
    unnamed x32 -> x28, local copies, waits for them, and re-layouts: 9.15 us -> 3.96 us
  transfers between devices with their start and end apart: 4 -> 5, of which waited for: 1 -> 2; matrix products, arithmetic and copies ran while one was open for 5% -> 4% of each run, Pallas kernels for 0% -> 0%
where the time goes in v5:
time: 486 us; the launch traced here: 485 us
  waiting for transfers between devices  209 us (43%)
  blocking collectives  195 us (40%)
  matrix products  35.5 us (7%)
  local copies, waits for them, and re-layouts  16 us (3%)
  other arithmetic  15 us (3%)
  between operations  14.1 us (3%)
    all_to_all x5, blocking collectives, scatter_a2a(): lax.all_to_all(p.reshape((size, p.shape[0] // size) + p.shape[1:]), axis_...  123 us
    all_gather x1, waiting for transfers between devices, on_device(): pair = lax.all_gather(own, TM, axis=2, tiled=True)  107 us
    reduce_scatter x1, waiting for transfers between devices, on_device(): grad_own = lax.psum_scatter(grad_own, 'ty', scatter_dimension=2, tiled=True)  102 us
    all_to_all x5, blocking collectives, gather_a2a(): y = lax.all_to_all(b, axis_name, 0, 0, tiled=True)  72.1 us
  transfers between devices with their start and end apart: 5, of which 2 were waited for; matrix products, arithmetic and copies ran while one was open for 4% of the time, Pallas kernels for 0%

profile of v5, /device:TPU:1, one launch (start us, length us, event | category | flops | bytes accessed | tf_op | source)
XLA Modules:
  0.0 485.0 jit_solution(11539162995851285736)
XLA Ops:
  9.5 107.0 %all-gather.2.cloned.1.call-done = bf16[2,2,512,2048]{3,2,1,0:T(8,128)(2,1)} async-done(((bf16[2,2,32,2048]{3,2,1,0:T(8,128)(2,1)}), bf16[2,2,512,2048]{3,2,1,0:T(8,128)(2,1)}) %all-gather.2.cloned.1.call-update) | async-done | bytes 8388624 | tf_op jit(solution)/shard_map/all_gather | solution.py:45
  116.4 2.7 slice.25
  119.3 2.4 fusion.20
  123.5 6.6 %add_convert_fusion = (bf16[2,512,2048]{2,1,0:T(8,128)(2,1)S(1)}, f32[2,2048,512]{1,2,0:T(8,128)}) fusion(bf16[2,2,512,2048]{3,2,1,0:T(8,128)(2,1)S(1)} %bitcast.105, bf16[512,512]{1,0:T(8,128)(2,1)S(1)} %copy-done.7), kind=kOutput, calls=%fused_computation.12 | convolution fusion | flops 2170552320 | bytes 21495808 | tf_op jit(solution)/shard_map/tl,blc->btc/dot_general | solution.py:48
  133.3 51.6 %all_to_all.50 = f32[4,256,2,512]{3,1,2,0:T(8,128)} all-to-all(f32[4,256,2,512]{3,1,2,0:T(8,128)S(1)} %copy.63), channel_id=1, replica_groups=mesh['zh'=2,'cx'=4,'tz'=4,'ty'=4,'dp'=2] {'cx'}, dimensions={0} | all-to-all | bytes 8388608 | tf_op jit(solution)/shard_map/all_to_all | solution.py:38
  184.9 2.8 reduce_sum.45
  187.8 21.7 %all_to_all.51 = f32[2,128,2,512]{3,1,2,0:T(8,128)S(1)} all-to-all(f32[2,128,2,512]{3,1,2,0:T(8,128)S(1)} %copy.65), channel_id=1, replica_groups=mesh['zh'=2,'cx'=4,'tz'=4,'ty'=4,'dp'=2] {'zh'}, dimensions={0} | all-to-all | bytes 2097152 | tf_op jit(solution)/shard_map/all_to_all | solution.py:38
  211.7 11.7 %all_to_all.52 = bf16[2,128,2,512]{3,1,2,0:T(8,128)(2,1)S(1)} all-to-all(bf16[2,128,2,512]{3,1,2,0:T(8,128)(2,1)S(1)} %broadcast_in_dim.16), channel_id=1, replica_groups=mesh['zh'=2,'cx'=4,'tz'=4,'ty'=4,'dp'=2] {'zh'}, dimensions={0} | all-to-all | bytes 1048576 | tf_op jit(solution)/shard_map/all_to_all | solution.py:33
  223.7 18.1 %all_to_all.53 = bf16[4,256,2,512]{3,1,2,0:T(8,128)(2,1)S(1)} all-to-all(bf16[4,256,2,512]{3,1,2,0:T(8,128)(2,1)S(1)} %broadcast_in_dim.35), channel_id=1, replica_groups=mesh['zh'=2,'cx'=4,'tz'=4,'ty'=4,'dp'=2] {'cx'}, dimensions={0} | all-to-all | bytes 4194304 | tf_op jit(solution)/shard_map/all_to_all | solution.py:33
  241.9 2.4 multiply_add_fusion.1
  244.4 7.6 %fusion.6 = bf16[2,512,2048]{2,1,0:T(8,128)(2,1)S(1)} fusion(f32[2,512,2048]{2,1,0:T(8,128)S(1)} %bitcast.90, f32[2,2048,512]{1,2,0:T(8,128)} %get-tuple-element.27), kind=kLoop, calls=%fused_computation.8 | loop fusion | flops 39845888 | bytes 20971520 | tf_op jit(solution)/shard_map/convert_element_type | solution.py:72
  252.0 2.9 bitcast_add_fusion
  254.9 3.8 copy.69
  258.8 102.3 %reduce-scatter.5.cloned.1.call-done = f32[2,4,1,32,2048]{4,3,1,0,2:T(8,128)} async-done(((f32[2,4,4,32,2048]{4,3,1,0,2:T(8,128)}), f32[2,4,1,32,2048]{4,3,1,0,2:T(8,128)}) %reduce-scatter.5.cloned.1.call-update) | async-done | bytes 2097168 | tf_op jit(solution)/shard_map/reduce_scatter | solution.py:76
  361.1 3.1 copy.70
  364.3 6.5 %fusion.27 = f32[2048,512]{1,0:T(8,128)} fusion(bf16[1024,2048]{1,0:T(8,128)(2,1)} %bitcast.108, bf16[1024,2,512]{2,0,1:T(8,128)(2,1)S(1)} %bitcast.98), kind=kOutput, calls=%fused_computation.30 | convolution fusion | flops 2147483648 | bytes 9437184 | tf_op jit(solution)/shard_map/rc,rh->ch/dot_general | solution.py:62
  371.1 6.5 %fusion.26 = f32[512,2048]{1,0:T(8,128)} fusion(bf16[1024,2048]{1,0:T(8,128)(2,1)} %bitcast.94, bf16[1024,2,512]{2,0,1:T(8,128)(2,1)S(1)} %bitcast.99), kind=kOutput, calls=%fused_computation.28 | convolution fusion | flops 2147483648 | bytes 9437184 | tf_op jit(solution)/shard_map/rh,rc->hc/dot_general | solution.py:63
  377.7 5.8 %fusion.23 = f32[2,256,512]{2,1,0:T(8,128)S(1)} fusion(bf16[2,256,2,2048]{3,1,0,2:T(8,128)(2,1)} %bitcast.96, bf16[2,2,512,2048]{3,2,1,0:T(8,128)(2,1)} %all-gather.2.cloned.1.call-done), kind=kOutput, calls=%fused_computation.26 | convolution fusion | flops 2147483648 | bytes 9437184 | tf_op jit(solution)/shard_map/btc,blc->tl/dot_general | solution.py:79
  383.5 4.9 %all_to_all.54 = f32[2,256,512]{2,1,0:T(8,128)S(1)} all-to-all(f32[2,256,512]{2,1,0:T(8,128)S(1)} %fusion.23), channel_id=1, replica_groups=mesh['zh'=2,'cx'=4,'tz'=4,'ty'=4,'dp'=2] {'dp'}, dimensions={0} | all-to-all | bytes 2097152 | tf_op jit(solution)/shard_map/all_to_all | solution.py:38
  388.6 29.0 %all_to_all.55 = f32[16,16,512]{2,1,0:T(8,128)S(1)} all-to-all(f32[16,16,512]{2,1,0:T(8,128)S(1)} %bitcast.106), channel_id=1, replica_groups=mesh['zh'=2,'cx'=4,'tz'=4,'ty'=4,'dp'=2] {'tz','ty'}, dimensions={0} | all-to-all | bytes 1048576 | tf_op jit(solution)/shard_map/all_to_all | solution.py:38
  417.6 15.3 %all_to_all.56 = f32[8,2,512]{2,1,0:T(2,128)S(1)} all-to-all(f32[8,2,512]{2,1,0:T(2,128)S(1)} %reshape.64), channel_id=1, replica_groups=mesh['zh'=2,'cx'=4,'tz'=4,'ty'=4,'dp'=2] {'zh','cx'}, dimensions={0} | all-to-all | bytes 65536 | tf_op jit(solution)/shard_map/all_to_all | solution.py:38
  432.9 11.4 %all_to_all.57 = f32[8,2,512]{2,1,0:T(2,128)S(1)} all-to-all(f32[8,2,512]{2,1,0:T(2,128)S(1)} %broadcast_in_dim.36), channel_id=1, replica_groups=mesh['zh'=2,'cx'=4,'tz'=4,'ty'=4,'dp'=2] {'zh','cx'}, dimensions={0} | all-to-all | bytes 65536 | tf_op jit(solution)/shard_map/all_to_all | solution.py:33
  444.4 20.8 %all_to_all.58 = f32[16,16,512]{2,1,0:T(8,128)S(1)} all-to-all(f32[16,16,512]{2,1,0:T(8,128)S(1)} %broadcast_in_dim.38), channel_id=1, replica_groups=mesh['zh'=2,'cx'=4,'tz'=4,'ty'=4,'dp'=2] {'tz','ty'}, dimensions={0} | all-to-all | bytes 1048576 | tf_op jit(solution)/shard_map/all_to_all | solution.py:33
  465.3 10.1 %all_to_all.59 = f32[2,256,512]{2,1,0:T(8,128)S(1)} all-to-all(f32[2,256,512]{2,1,0:T(8,128)S(1)} %broadcast_in_dim.40), channel_id=1, replica_groups=mesh['zh'=2,'cx'=4,'tz'=4,'ty'=4,'dp'=2] {'dp'}, dimensions={0} | all-to-all | bytes 2097152 | tf_op jit(solution)/shard_map/all_to_all | solution.py:33
  (64 shorter events, 13.9 us)
Async XLA Ops:
  7.2 122.9 %copy-start = (bf16[2048,512]{1,0:T(8,128)(2,1)S(1)}, bf16[2048,512]{1,0:T(8,128)(2,1)}, u32[]{:S(2)}) copy-start(bf16[2048,512]{1,0:T(8,128)(2,1)} %param.7) | copy-start | bytes 6291460
  7.2 109.3 %all-gather.2.cloned.1.call-start = ((), (), s32[]{:S(2)}) async-start(), calls=%async_computation.14 | async-start | bytes 8912896 | tf_op jit(solution)/shard_map/all_gather | solution.py:45
  9.4 351.7 %reduce-scatter.5.cloned.1.call-start = ((), (), s32[]{:S(2)}) async-start(), calls=%async_computation.15 | async-start | bytes 10485760 | tf_op jit(solution)/shard_map/reduce_scatter | solution.py:76
  116.4 2.9 copy-start.9
  116.4 5.3 %slice-start = ((s8[8388608]{0:T(1024)(128)(4,1)}), s8[4194304]{0:T(1024)(128)(4,1)S(1)}, s32[]{:S(2)}) async-start(s8[8388608]{0:T(1024)(128)(4,1)} %bitcast.104), calls=%async_computation.19 | async-start | bytes 8388608
  119.1 2.6 copy-start.2
  119.3 4.2 slice-start.1
  119.3 4.2 copy-start.7
  130.1 2.3 copy-start.10
  223.7 18.3 %copy-start.3 = (bf16[1,2,512,2048]{3,2,1,0:T(8,128)(2,1)S(1)}, bf16[1,2,512,2048]{3,2,1,0:T(8,128)(2,1)}, u32[]{:S(2)}) copy-start(bf16[1,2,512,2048]{3,2,1,0:T(8,128)(2,1)} %copy-done.2) | copy-start | bytes 12582916
  241.9 2.4 copy-start.5
  244.4 7.6 %copy-start.8 = (bf16[512,512]{1,0:T(8,128)(2,1)S(1)}, bf16[512,512]{1,0:T(8,128)(2,1)}, u32[]{:S(2)}) copy-start(bf16[512,512]{1,0:T(8,128)(2,1)} %param.9) | copy-start | bytes 1572868
  252.0 2.9 copy-start.4
  258.7 105.6 %copy-start.6 = (bf16[4,256,2,512]{3,1,0,2:T(8,128)(2,1)S(1)}, bf16[4,256,2,512]{3,1,0,2:T(8,128)(2,1)}, u32[]{:S(2)}) copy-start(bf16[4,256,2,512]{3,1,0,2:T(8,128)(2,1)} %copy-done.5) | copy-start | bytes 6291460
  258.7 216.7 %reduce-scatter.7.cloned.1.call-start = ((), (), s32[]{:S(2)}) async-start(), calls=%async_computation.16 | async-start | bytes 2621440 | tf_op jit(solution)/shard_map/reduce_scatter | solution.py:77
  364.2 113.2 %reduce-scatter.9.cloned.1.call-start = ((), (), s32[]{:S(2)}) async-start(), calls=%async_computation.17 | async-start | bytes 6291456 | tf_op jit(solution)/shard_map/reduce_scatter | solution.py:65
  370.9 106.6 %reduce-scatter.11.cloned.1.call-start = ((), (), s32[]{:S(2)}) async-start(), calls=%async_computation.18 | async-start | bytes 6291456 | tf_op jit(solution)/shard_map/reduce_scatter | solution.py:66
  444.3 34.1 %copy-start.1 = (bf16[2048,512]{1,0:T(8,128)(2,1)S(1)}, bf16[2048,512]{1,0:T(8,128)(2,1)}, u32[]{:S(2)}) copy-start(bf16[2048,512]{1,0:T(8,128)(2,1)} %param.7) | copy-start | bytes 6291460
Sparse Core Ops, SparseCore 0:
  10.4 106.0 all-gather.1
  258.8 102.1 reduce-scatter.4
  364.4 56.6 reduce-scatter.6
  424.1 19.8 reduce-scatter.8
  446.9 18.7 reduce-scatter.10

commit v6 on v3

--- a/solution.py
+++ b/solution.py
@@ -92,7 +92,7 @@
         tm=tm,
         chan=chan,
         chan_near=chan // far,
-        stages=((("dp",), dp), (TM, tm), (CHAN, chan)),
+        stages=((CHAN + TM + ("dp",), mesh.size),),
     )
     token = P(TM, "dp", CHAN)
     return jax.shard_map(

time: 452 us -> 455 us (level)
  blocking collectives: 265 us -> 253 us
  local copies, waits for them, and re-layouts: 14.3 us -> 23.5 us
    all_to_all x5 -> x3, blocking collectives: 182 us -> 160 us  [scatter_a2a(): lax.all_to_all(p.reshape((size, p.shape[0] // size) + p.shape[1:]), axis_...]
    all_to_all x5 -> x3, blocking collectives: 82.3 us -> 93.2 us  [gather_a2a(): y = lax.all_to_all(b, axis_name, 0, 0, tiled=True)]
    dot_general x0 -> x2, local copies, waits for them, and re-layouts: none -> 8.45 us  [on_device(): jnp.einsum('btc,blc->tl', gate, whole_x, preferred_element_type=jnp.float32)]
    unnamed x32 -> x31, local copies, waits for them, and re-layouts: 9.15 us -> 8.19 us
  transfers between devices with their start and end apart: 4 -> 4, of which waited for: 1 -> 2; matrix products, arithmetic and copies ran while one was open for 5% -> 7% of each run, Pallas kernels for 0% -> 0%
where the time goes in v6:
time: 455 us; the launch traced here: 454 us
  blocking collectives  253 us (56%)
  waiting for transfers between devices  110 us (24%)
  matrix products  39.3 us (9%)
  local copies, waits for them, and re-layouts  23.5 us (5%)
  between operations  14 us (3%)
  other arithmetic  13.1 us (3%)
    all_to_all x3, blocking collectives, scatter_a2a(): lax.all_to_all(p.reshape((size, p.shape[0] // size) + p.shape[1:]), axis_...  160 us
    all_gather x1, waiting for transfers between devices, on_device(): pair = lax.all_gather(own, TM, axis=2, tiled=True)  107 us
    all_to_all x3, blocking collectives, gather_a2a(): y = lax.all_to_all(b, axis_name, 0, 0, tiled=True)  93.2 us
  transfers between devices with their start and end apart: 4, of which 2 were waited for; matrix products, arithmetic and copies ran while one was open for 7% of the time, Pallas kernels for 0%

profile of v6, /device:TPU:1, one launch (start us, length us, event | category | flops | bytes accessed | tf_op | source)
XLA Modules:
  0.0 453.9 jit_solution(17195879354433040872)
XLA Ops:
  9.5 107.0 %all-gather.2.cloned.1.call-done = bf16[2,2,512,2048]{3,2,1,0:T(8,128)(2,1)} async-done(((bf16[2,2,32,2048]{3,2,1,0:T(8,128)(2,1)}), bf16[2,2,512,2048]{3,2,1,0:T(8,128)(2,1)}) %all-gather.2.cloned.1.call-update) | async-done | bytes 8388624 | tf_op jit(solution)/shard_map/all_gather | solution.py:44
  116.4 2.7 slice.25
  119.3 2.4 fusion.21
  121.7 1.7 slice-done.3
  123.5 6.6 %add_convert_fusion = (bf16[2,512,2048]{2,1,0:T(8,128)(2,1)S(1)}, f32[2,2048,512]{1,2,0:T(8,128)}) fusion(bf16[2,2,512,2048]{3,2,1,0:T(8,128)(2,1)S(1)} %bitcast.95, bf16[512,512]{1,0:T(8,128)(2,1)S(1)} %copy-done.7), kind=kOutput, calls=%fused_computation.12 | convolution fusion | flops 2170552320 | bytes 21495808 | tf_op jit(solution)/shard_map/tl,blc->btc/dot_general | solution.py:47
  130.1 2.3 fusion.18
  133.3 51.6 %all_to_all.30 = f32[4,256,2,512]{3,1,2,0:T(8,128)} all-to-all(f32[4,256,2,512]{3,1,2,0:T(8,128)S(1)} %copy.44), channel_id=1, replica_groups=mesh['zh'=2,'cx'=4,'tz'=4,'ty'=4,'dp'=2] {'cx'}, dimensions={0} | all-to-all | bytes 8388608 | tf_op jit(solution)/shard_map/all_to_all | solution.py:37
  185.0 2.8 reduce_sum.27
  187.8 21.6 %all_to_all.31 = f32[2,128,2,512]{3,1,2,0:T(8,128)S(1)} all-to-all(f32[2,128,2,512]{3,1,2,0:T(8,128)S(1)} %copy.46), channel_id=1, replica_groups=mesh['zh'=2,'cx'=4,'tz'=4,'ty'=4,'dp'=2] {'zh'}, dimensions={0} | all-to-all | bytes 2097152 | tf_op jit(solution)/shard_map/all_to_all | solution.py:37
  211.6 11.7 %all_to_all.32 = bf16[2,128,2,512]{3,1,2,0:T(8,128)(2,1)S(1)} all-to-all(bf16[2,128,2,512]{3,1,2,0:T(8,128)(2,1)S(1)} %broadcast_in_dim.8), channel_id=1, replica_groups=mesh['zh'=2,'cx'=4,'tz'=4,'ty'=4,'dp'=2] {'zh'}, dimensions={0} | all-to-all | bytes 1048576 | tf_op jit(solution)/shard_map/all_to_all | solution.py:32
  223.6 18.1 %all_to_all.33 = bf16[4,256,2,512]{3,1,2,0:T(8,128)(2,1)S(1)} all-to-all(bf16[4,256,2,512]{3,1,2,0:T(8,128)(2,1)S(1)} %broadcast_in_dim.10), channel_id=1, replica_groups=mesh['zh'=2,'cx'=4,'tz'=4,'ty'=4,'dp'=2] {'cx'}, dimensions={0} | all-to-all | bytes 4194304 | tf_op jit(solution)/shard_map/all_to_all | solution.py:32
  241.9 2.4 multiply_add_fusion.1
  246.1 5.5 %fusion.6 = bf16[2,512,2048]{2,1,0:T(8,128)(2,1)S(1)} fusion(f32[2,512,2048]{2,1,0:T(8,128)S(1)} %bitcast.82, f32[2,2048,512]{1,2,0:T(8,128)S(1)} %bitcast.88), kind=kLoop, calls=%fused_computation.8 | loop fusion | flops 39845888 | bytes 20971520 | tf_op jit(solution)/shard_map/convert_element_type | solution.py:71
  251.6 1.9 copy-done.2
  253.5 6.0 %bitcast_add_fusion = f32[2,512,2048]{2,1,0:T(8,128)} fusion(f32[2,512,2048]{2,1,0:T(8,128)S(1)} %bitcast.83, bf16[2,512,2048]{2,1,0:T(8,128)(2,1)S(1)} %fusion.6, bf16[512,512]{1,0:T(8,128)(2,1)S(1)} %copy-done.8), kind=kOutput, calls=%fused_computation.9 | convolution fusion | flops 2149580800 | bytes 21495808 | tf_op jit(solution)/shard_map/tl,btc->blc/dot_general | solution.py:72
  259.6 1.5 copy-done.6
  261.1 6.5 %fusion.30 = f32[2048,512]{1,0:T(8,128)} fusion(bf16[1024,2048]{1,0:T(8,128)(2,1)} %bitcast.97, bf16[1024,2,512]{2,0,1:T(8,128)(2,1)S(1)} %bitcast.90), kind=kOutput, calls=%fused_computation.31 | convolution fusion | flops 2147483648 | bytes 9437184 | tf_op jit(solution)/shard_map/rc,rh->ch/dot_general | solution.py:61
  267.9 6.5 %fusion.29 = f32[512,2048]{1,0:T(8,128)} fusion(bf16[1024,2048]{1,0:T(8,128)(2,1)} %bitcast.85, bf16[1024,2,512]{2,0,1:T(8,128)(2,1)S(1)} %bitcast.91), kind=kOutput, calls=%fused_computation.29 | convolution fusion | flops 2147483648 | bytes 9437184 | tf_op jit(solution)/shard_map/rh,rc->hc/dot_general | solution.py:62
  274.5 7.6 %dot_general.48 = bf16[256,2,2,2048]{3,1,0,2:T(2,128)(2,1)} reshape(bf16[512,2,2048]{2,0,1:T(8,128)(2,1)} %bitcast.81) | data formatting | bytes 8388608 | tf_op jit(solution)/shard_map/btc,blc->tl/dot_general | solution.py:75
  282.1 6.5 %fusion.24 = f32[256,2,512]{2,0,1:T(8,128)S(1)} fusion(bf16[2,2,512,2048]{3,2,1,0:T(8,128)(2,1)} %all-gather.2.cloned.1.call-done, bf16[256,2,2,2048]{3,1,0,2:T(2,128)(2,1)} %dot_general.48), kind=kOutput, calls=%fused_computation.27 | convolution fusion | flops 2147483648 | bytes 9437184 | tf_op jit(solution)/shard_map/btc,blc->tl/dot_general | solution.py:75
  289.4 86.9 %all_to_all.34 = f32[256,2,512]{2,1,0:T(2,128)S(1)} all-to-all(f32[256,2,512]{2,1,0:T(2,128)S(1)} %copy.52), channel_id=1, replica_groups=mesh['zh'=2,'cx'=4,'tz'=4,'ty'=4,'dp'=2] {'zh','cx','tz','ty','dp'}, dimensions={0} | all-to-all | bytes 2097152 | tf_op jit(solution)/shard_map/all_to_all | solution.py:37
  377.0 63.3 %all_to_all.35 = f32[256,2,512]{2,1,0:T(2,128)S(1)} all-to-all(f32[256,2,512]{2,1,0:T(2,128)S(1)} %broadcast_in_dim.22), channel_id=1, replica_groups=mesh['zh'=2,'cx'=4,'tz'=4,'ty'=4,'dp'=2] {'zh','cx','tz','ty','dp'}, dimensions={0} | all-to-all | bytes 2097152 | tf_op jit(solution)/shard_map/all_to_all | solution.py:32
  440.3 1.7 reshape.49
  444.1 3.3 reduce-scatter.8.cloned.1.call-done
  (56 shorter events, 11.6 us)
Async XLA Ops:
  7.2 122.9 %copy-start = (bf16[2048,512]{1,0:T(8,128)(2,1)S(1)}, bf16[2048,512]{1,0:T(8,128)(2,1)}, u32[]{:S(2)}) copy-start(bf16[2048,512]{1,0:T(8,128)(2,1)} %param.7) | copy-start | bytes 6291460
  7.2 109.3 %all-gather.2.cloned.1.call-start = ((), (), s32[]{:S(2)}) async-start(), calls=%async_computation.9 | async-start | bytes 8912896 | tf_op jit(solution)/shard_map/all_gather | solution.py:44
  9.4 432.6 %reduce-scatter.4.cloned.1.call-start = ((), (), s32[]{:S(2)}) async-start(), calls=%async_computation.10 | async-start | bytes 8912896 | tf_op jit(solution)/shard_map/reduce_scatter | solution.py:73
  116.4 2.9 copy-start.9
  116.4 5.3 %slice-start.2 = ((s8[8388608]{0:T(1024)(128)(4,1)}), s8[4194304]{0:T(1024)(128)(4,1)S(1)}, s32[]{:S(2)}) async-start(s8[8388608]{0:T(1024)(128)(4,1)} %bitcast.94), calls=%async_computation.15 | async-start | bytes 8388608
  119.1 2.6 copy-start.3
  119.3 4.2 slice-start.3
  119.3 4.2 copy-start.7
  130.1 2.3 copy-start.10
  223.6 18.3 %copy-start.4 = (bf16[1,2,512,2048]{3,2,1,0:T(8,128)(2,1)S(1)}, bf16[1,2,512,2048]{3,2,1,0:T(8,128)(2,1)}, u32[]{:S(2)}) copy-start(bf16[1,2,512,2048]{3,2,1,0:T(8,128)(2,1)} %copy-done.3) | copy-start | bytes 12582916
  241.9 2.5 copy-start.5
  241.9 2.9 slice-start
  241.9 4.2 slice-start.1
  246.1 7.4 %copy-start.8 = (bf16[512,512]{1,0:T(8,128)(2,1)S(1)}, bf16[512,512]{1,0:T(8,128)(2,1)}, u32[]{:S(2)}) copy-start(bf16[512,512]{1,0:T(8,128)(2,1)} %param.9) | copy-start | bytes 1572868
  251.6 1.9 copy-start.2
  259.5 1.6 copy-start.6
  259.5 184.6 %reduce-scatter.6.cloned.1.call-start = ((), (), s32[]{:S(2)}) async-start(), calls=%async_computation.11 | async-start | bytes 6291456 | tf_op jit(solution)/shard_map/reduce_scatter | solution.py:64
  267.7 179.7 %reduce-scatter.8.cloned.1.call-start = ((), (), s32[]{:S(2)}) async-start(), calls=%async_computation.12 | async-start | bytes 6291456 | tf_op jit(solution)/shard_map/reduce_scatter | solution.py:65
  289.4 158.0 %copy-start.1 = (bf16[2048,512]{1,0:T(8,128)(2,1)S(1)}, bf16[2048,512]{1,0:T(8,128)(2,1)}, u32[]{:S(2)}) copy-start(bf16[2048,512]{1,0:T(8,128)(2,1)} %param.7) | copy-start | bytes 6291460
Sparse Core Ops, SparseCore 0:
  10.4 106.0 all-gather.1
  259.6 142.4 reduce-scatter.3
  405.2 20.3 reduce-scatter.5
  428.6 18.7 reduce-scatter.7

commit v7 on v3

--- a/solution.py
+++ b/solution.py
@@ -52,12 +52,15 @@
     grad_rows = whole_dy.reshape(rows, width_dev)
     hidden_part = jnp.dot(mixed_rows, w_in, preferred_element_type=jnp.float32)
     hgrad_part = jnp.einsum("rc,hc->rh", grad_rows, w_out, preferred_element_type=jnp.float32)
-    summed = scatter_a2a(jnp.stack([hidden_part, hgrad_part], 1), "cx", chan_near)
-    summed = scatter_a2a(summed, "zh", chan // chan_near)
-    act_rows, pre_grad_rows = hidden_finish(summed[:, 0], summed[:, 1])
-    fin = gather_a2a(jnp.stack([act_rows, pre_grad_rows], 1), "zh", chan // chan_near)
-    fin = gather_a2a(fin, "cx", chan_near)
-    activation, pre_grad = fin[:, 0], fin[:, 1]
+    hidden_pre = lax.psum_scatter(hidden_part, "cx", scatter_dimension=0, tiled=True)
+    hidden_pre = lax.psum_scatter(hidden_pre, "zh", scatter_dimension=0, tiled=True)
+    hidden_grad = scatter_a2a(hgrad_part, "cx", chan_near)
+    hidden_grad = scatter_a2a(hidden_grad, "zh", chan // chan_near)
+    act_rows, pre_grad_rows = hidden_finish(hidden_pre, hidden_grad)
+    activation = lax.all_gather(act_rows, "zh", axis=0, tiled=True)
+    activation = lax.all_gather(activation, "cx", axis=0, tiled=True)
+    pre_grad = gather_a2a(pre_grad_rows, "zh", chan // chan_near)
+    pre_grad = gather_a2a(pre_grad, "cx", chan_near)
     win_part = jnp.einsum("rc,rh->ch", mixed_rows, pre_grad, preferred_element_type=jnp.float32)
     wout_part = jnp.einsum("rh,rc->hc", activation, grad_rows, preferred_element_type=jnp.float32)
     grad_w_in, grad_w_out = (

time: 452 us -> 452 us (level)
  blocking collectives: 265 us -> 193 us
  waiting for transfers between devices: 107 us -> 163 us
  starting transfers between devices: 0.38 us -> 8.69 us
  matrix products: 38.6 us -> 46 us
    all_to_all x5 -> x4, blocking collectives: 182 us -> 105 us  [scatter_a2a(): lax.all_to_all(p.reshape((size, p.shape[0] // size) + p.shape[1:]), axis_...]
    reduce_scatter x0 -> x2, waiting for transfers between devices: none -> 42.6 us  [the longest x1 27.1 us: on_device(): lax.psum_scatter(hidden_part, 'cx', scatter_dimension=0, tiled=True)]
    all_to_all x0 -> x2, waiting for transfers between devices: none -> 12.9 us  [the longest x1 10.9 us: scatter_a2a(): lax.all_to_all(p.reshape((size, p.shape[0] // size) + p.shape[1:]), axis_...]
    all_gather x0 -> x1, blocking collectives: none -> 8.5 us  [on_device(): activation = lax.all_gather(act_rows, 'zh', axis=0, tiled=True)]
    all_to_all x0 -> x2, starting transfers between devices: none -> 8 us  [the longest x1 4.49 us: scatter_a2a(): lax.all_to_all(p.reshape((size, p.shape[0] // size) + p.shape[1:]), axis_...]
    all_to_all x5 -> x4, blocking collectives: 82.3 us -> 79.4 us  [gather_a2a(): y = lax.all_to_all(b, axis_name, 0, 0, tiled=True)]
    unnamed x32 -> x16, local copies, waits for them, and re-layouts: 9.15 us -> 7.8 us
  transfers between devices with their start and end apart: 4 -> 9, of which waited for: 1 -> 5; matrix products, arithmetic and copies ran while one was open for 5% -> 11% of each run, Pallas kernels for 0% -> 0%
where the time goes in v7:
time: 452 us; the launch traced here: 451 us
  blocking collectives  193 us (43%)
  waiting for transfers between devices  163 us (36%)
  matrix products  46 us (10%)
  between operations  14.3 us (3%)
  other arithmetic  13.5 us (3%)
  local copies, waits for them, and re-layouts  13.1 us (3%)
  starting transfers between devices  8.69 us (2%)
    all_gather x1, waiting for transfers between devices, on_device(): pair = lax.all_gather(own, TM, axis=2, tiled=True)  107 us
    all_to_all x4, blocking collectives, scatter_a2a(): lax.all_to_all(p.reshape((size, p.shape[0] // size) + p.shape[1:]), axis_...  105 us
    all_to_all x4, blocking collectives, gather_a2a(): y = lax.all_to_all(b, axis_name, 0, 0, tiled=True)  79.4 us
    reduce_scatter x1, waiting for transfers between devices, on_device(): lax.psum_scatter(hidden_part, 'cx', scatter_dimension=0, tiled=True)  27.1 us
    reduce_scatter x1, waiting for transfers between devices, on_device(): lax.psum_scatter(hidden_pre, 'zh', scatter_dimension=0, tiled=True)  15.4 us
    all_to_all x1, waiting for transfers between devices, scatter_a2a(): lax.all_to_all(p.reshape((size, p.shape[0] // size) + p.shape[1:]), axis_...  10.9 us
  transfers between devices with their start and end apart: 9, of which 5 were waited for; matrix products, arithmetic and copies ran while one was open for 11% of the time, Pallas kernels for 0%

profile of v7, /device:TPU:1, one launch (start us, length us, event | category | flops | bytes accessed | tf_op | source)
XLA Modules:
  0.0 451.3 jit_solution(7848856808852410994)
XLA Ops:
  9.5 107.0 %all-gather.3.cloned.1.call-done = bf16[2,2,512,2048]{3,2,1,0:T(8,128)(2,1)} async-done(((bf16[2,2,32,2048]{3,2,1,0:T(8,128)(2,1)}), bf16[2,2,512,2048]{3,2,1,0:T(8,128)(2,1)}) %all-gather.3.cloned.1.call-update) | async-done | bytes 8388624 | tf_op jit(solution)/shard_map/all_gather | solution.py:44
  116.4 8.8 %add_convert_fusion = (bf16[2,512,2048]{2,1,0:T(8,128)(2,1)S(1)}, f32[2,2048,512]{1,2,0:T(8,128)}) fusion(bf16[2,2,512,2048]{3,2,1,0:T(8,128)(2,1)} %all-gather.3.cloned.1.call-done, bf16[512,512]{1,0:T(8,128)(2,1)} %param.9), kind=kOutput, calls=%fused_computation.12 | convolution fusion | flops 2170552320 | bytes 21495808 | tf_op jit(solution)/shard_map/tl,blc->btc/dot_general | solution.py:47
  127.2 3.6 fusion.27
  135.5 3.7 fusion.13
  139.2 4.5 all-to-all-start
  143.7 27.1 %reduce-scatter.6.cloned.1.call-done = f32[256,512]{1,0:T(8,128)} async-done(((f32[1024,512]{1,0:T(8,128)}), f32[256,512]{1,0:T(8,128)}) %reduce-scatter.6.cloned.1.call-update) | async-done | bytes 524304 | tf_op jit(solution)/shard_map/reduce_scatter | solution.py:55
  170.9 10.9 %all-to-all-done = f32[4,256,512]{2,1,0:T(8,128)} async-done(((f32[4,256,512]{2,1,0:T(8,128)}), f32[4,256,512]{2,1,0:T(8,128)}, u32[]{:S(2)}, u32[]{:S(2)}) %all-to-all-start) | async-done | bytes 2097184 | tf_op jit(solution)/shard_map/all_to_all | solution.py:37
  183.7 19.7 %all_to_all.50 = f32[2,128,512]{2,1,0:T(8,128)S(1)} all-to-all(f32[2,128,512]{2,1,0:T(8,128)S(1)} %bitcast.80), channel_id=1, replica_groups=mesh['zh'=2,'cx'=4,'tz'=4,'ty'=4,'dp'=2] {'zh'}, dimensions={0} | all-to-all | bytes 1048576 | tf_op jit(solution)/shard_map/all_to_all | solution.py:37
  203.4 15.4 %reduce-scatter.8.cloned.1.call-done = f32[128,512]{1,0:T(8,128)} async-done(((f32[256,512]{1,0:T(8,128)}), f32[128,512]{1,0:T(8,128)}) %reduce-scatter.8.cloned.1.call-update) | async-done | bytes 262160 | tf_op jit(solution)/shard_map/reduce_scatter | solution.py:56
  220.0 11.0 %all_to_all.51 = bf16[2,128,512]{2,1,0:T(8,128)(2,1)S(1)} all-to-all(bf16[2,128,512]{2,1,0:T(8,128)(2,1)S(1)} %broadcast_in_dim.16), channel_id=1, replica_groups=mesh['zh'=2,'cx'=4,'tz'=4,'ty'=4,'dp'=2] {'zh'}, dimensions={0} | all-to-all | bytes 524288 | tf_op jit(solution)/shard_map/all_to_all | solution.py:32
  232.0 3.5 all-to-all-start.3
  235.6 8.5 %all_gather.10 = bf16[256,512]{1,0:T(8,128)(2,1)} all-gather(bf16[128,512]{1,0:T(8,128)(2,1)S(1)} %get-tuple-element.16), channel_id=1, replica_groups=mesh['zh'=2,'cx'=4,'tz'=4,'ty'=4,'dp'=2] {'zh'}, dimensions={0}, use_global_device_ids=true | all-gather | bytes 393216 | tf_op jit(solution)/shard_map/all_gather | solution.py:60
  246.3 4.6 %multiply_add_fusion.1 = f32[1024,2048]{1,0:T(8,128)S(1)} fusion(bf16[1024,2048]{1,0:T(8,128)(2,1)} %bitcast.74, bf16[1024,512]{1,0:T(8,128)(2,1)S(1)} %bitcast.82, bf16[2048,512]{1,0:T(8,128)(2,1)S(1)} %copy-done), kind=kOutput, calls=%fused_computation.11 | convolution fusion | flops 2153775104 | bytes 15728640 | tf_op jit(solution)/shard_map/rh,ch->rc/dot_general | solution.py:70
  250.9 7.6 %fusion.6 = bf16[2,512,2048]{2,1,0:T(8,128)(2,1)S(1)} fusion(f32[2,512,2048]{2,1,0:T(8,128)S(1)} %bitcast.71, f32[2,2048,512]{1,2,0:T(8,128)} %get-tuple-element.19), kind=kLoop, calls=%fused_computation.8 | loop fusion | flops 39845888 | bytes 20971520 | tf_op jit(solution)/shard_map/convert_element_type | solution.py:74
  260.4 6.0 %bitcast_add_fusion = f32[2,512,2048]{2,1,0:T(8,128)} fusion(f32[2,512,2048]{2,1,0:T(8,128)S(1)} %bitcast.72, bf16[2,512,2048]{2,1,0:T(8,128)(2,1)S(1)} %fusion.6, bf16[512,512]{1,0:T(8,128)(2,1)S(1)} %copy-done.4), kind=kOutput, calls=%fused_computation.9 | convolution fusion | flops 2149580800 | bytes 21495808 | tf_op jit(solution)/shard_map/tl,btc->blc/dot_general | solution.py:75
  266.4 6.6 %fusion.28 = f32[2048,512]{1,0:T(8,128)} fusion(bf16[1024,2048]{1,0:T(8,128)(2,1)} %bitcast.85, bf16[1024,512]{1,0:T(8,128)(2,1)S(1)} %bitcast.83), kind=kOutput, calls=%fused_computation.39 | convolution fusion | flops 2147483648 | bytes 9437184 | tf_op jit(solution)/shard_map/rc,rh->ch/dot_general | solution.py:64
  273.3 6.9 %fusion.29 = f32[512,2048]{1,0:T(8,128)} fusion(bf16[1024,512]{1,0:T(8,128)(2,1)} %all-gather.5.cloned.1.call-done, bf16[1024,2048]{1,0:T(8,128)(2,1)} %bitcast.75), kind=kOutput, calls=%fused_computation.40 | convolution fusion | flops 2147483648 | bytes 9437184 | tf_op jit(solution)/shard_map/rh,rc->hc/dot_general | solution.py:65
  280.2 6.0 %fusion.15 = f32[2,256,512]{2,1,0:T(8,128)S(1)} fusion(bf16[2,256,2,2048]{3,1,0,2:T(8,128)(2,1)} %bitcast.76, bf16[2,2,512,2048]{3,2,1,0:T(8,128)(2,1)} %all-gather.3.cloned.1.call-done), kind=kOutput, calls=%fused_computation.21 | convolution fusion | flops 2147483648 | bytes 9437184 | tf_op jit(solution)/shard_map/btc,blc->tl/dot_general | solution.py:78
  286.2 9.4 %all_to_all.52 = f32[2,256,512]{2,1,0:T(8,128)S(1)} all-to-all(f32[2,256,512]{2,1,0:T(8,128)S(1)} %fusion.15), channel_id=1, replica_groups=mesh['zh'=2,'cx'=4,'tz'=4,'ty'=4,'dp'=2] {'dp'}, dimensions={0} | all-to-all | bytes 2097152 | tf_op jit(solution)/shard_map/all_to_all | solution.py:37
  296.5 48.1 %all_to_all.53 = f32[16,16,512]{2,1,0:T(8,128)S(1)} all-to-all(f32[16,16,512]{2,1,0:T(8,128)} %bitcast.79), channel_id=1, replica_groups=mesh['zh'=2,'cx'=4,'tz'=4,'ty'=4,'dp'=2] {'tz','ty'}, dimensions={0} | all-to-all | bytes 1048576 | tf_op jit(solution)/shard_map/all_to_all | solution.py:37
  344.6 28.2 %all_to_all.54 = f32[8,2,512]{2,1,0:T(2,128)S(1)} all-to-all(f32[8,2,512]{2,1,0:T(2,128)S(1)} %reshape.44), channel_id=1, replica_groups=mesh['zh'=2,'cx'=4,'tz'=4,'ty'=4,'dp'=2] {'zh','cx'}, dimensions={0} | all-to-all | bytes 65536 | tf_op jit(solution)/shard_map/all_to_all | solution.py:37
  372.9 11.7 %all_to_all.55 = f32[8,2,512]{2,1,0:T(2,128)S(1)} all-to-all(f32[8,2,512]{2,1,0:T(2,128)S(1)} %broadcast_in_dim.36), channel_id=1, replica_groups=mesh['zh'=2,'cx'=4,'tz'=4,'ty'=4,'dp'=2] {'zh','cx'}, dimensions={0} | all-to-all | bytes 65536 | tf_op jit(solution)/shard_map/all_to_all | solution.py:32
  384.7 47.0 %all_to_all.56 = f32[16,16,512]{2,1,0:T(8,128)S(1)} all-to-all(f32[16,16,512]{2,1,0:T(8,128)S(1)} %broadcast_in_dim.38), channel_id=1, replica_groups=mesh['zh'=2,'cx'=4,'tz'=4,'ty'=4,'dp'=2] {'tz','ty'}, dimensions={0} | all-to-all | bytes 1048576 | tf_op jit(solution)/shard_map/all_to_all | solution.py:32
  431.8 9.6 %all_to_all.57 = f32[2,256,512]{2,1,0:T(8,128)S(1)} all-to-all(f32[2,256,512]{2,1,0:T(8,128)S(1)} %broadcast_in_dim.40), channel_id=1, replica_groups=mesh['zh'=2,'cx'=4,'tz'=4,'ty'=4,'dp'=2] {'dp'}, dimensions={0} | all-to-all | bytes 2097152 | tf_op jit(solution)/shard_map/all_to_all | solution.py:32
  (52 shorter events, 21.8 us)
Async XLA Ops:
  7.2 120.0 %copy-start = (bf16[2048,512]{1,0:T(8,128)(2,1)S(1)}, bf16[2048,512]{1,0:T(8,128)(2,1)}, u32[]{:S(2)}) copy-start(bf16[2048,512]{1,0:T(8,128)(2,1)} %param.7) | copy-start | bytes 6291460
  7.2 109.3 %all-gather.3.cloned.1.call-start = ((), (), s32[]{:S(2)}) async-start(), calls=%async_computation.15 | async-start | bytes 8912896 | tf_op jit(solution)/shard_map/all_gather | solution.py:44
  9.4 161.4 %reduce-scatter.6.cloned.1.call-start = ((), (), s32[]{:S(2)}) async-start(), calls=%async_computation.16 | async-start | bytes 2621440 | tf_op jit(solution)/shard_map/reduce_scatter | solution.py:55
  125.2 2.0 copy-start.6
  130.9 4.6 %copy-start.5 = (bf16[512,2048]{1,0:T(8,128)(2,1)S(1)}, bf16[512,2048]{1,0:T(8,128)(2,1)}, u32[]{:S(2)}) copy-start(bf16[512,2048]{1,0:T(8,128)(2,1)} %param.8) | copy-start | bytes 6291460
  133.5 1.9 copy-start.2
  139.2 42.6 %all-to-all-start = ((f32[4,256,512]{2,1,0:T(8,128)}), f32[4,256,512]{2,1,0:T(8,128)}, u32[]{:S(2)}, u32[]{:S(2)}) async-start(f32[4,256,512]{2,1,0:T(8,128)} %fusion.13), calls=%async_computation | async-start | bytes 4194304 | tf_op jit(solution)/shard_map/all_to_all | solution.py:37
  143.7 75.2 %reduce-scatter.8.cloned.1.call-start = ((), (), s32[]{:S(2)}) async-start(), calls=%async_computation.17 | async-start | bytes 786432 | tf_op jit(solution)/shard_map/reduce_scatter | solution.py:56
  232.0 14.3 %all-to-all-start.3 = ((bf16[4,256,512]{2,1,0:T(8,128)(2,1)}), bf16[4,256,512]{2,1,0:T(8,128)(2,1)S(1)}, u32[]{:S(2)}, u32[]{:S(2)}) async-start(bf16[4,256,512]{2,1,0:T(8,128)(2,1)} %broadcast_in_dim.35), calls=%async_computation.5 | async-start | bytes 2097152 | tf_op jit(solution)/shard_map/all_to_all | solution.py:32
  235.5 37.8 %all-gather.5.cloned.1.call-start = ((), (), s32[]{:S(2)}) async-start(), calls=%async_computation.20 | async-start | bytes 1310720 | tf_op jit(solution)/shard_map/all_gather | solution.py:61
  244.1 197.4 %reduce-scatter.10.cloned.1.call-start = ((), (), s32[]{:S(2)}) async-start(), calls=%async_computation.18 | async-start | bytes 8912896 | tf_op jit(solution)/shard_map/reduce_scatter | solution.py:76
  250.9 9.5 %copy-start.4 = (bf16[512,512]{1,0:T(8,128)(2,1)S(1)}, bf16[512,512]{1,0:T(8,128)(2,1)}, u32[]{:S(2)}) copy-start(bf16[512,512]{1,0:T(8,128)(2,1)} %param.9) | copy-start | bytes 1572868
  258.5 1.9 copy-start.3
  266.4 177.1 %reduce-scatter.12.cloned.1.call-start = ((), (), s32[]{:S(2)}) async-start(), calls=%async_computation.19 | async-start | bytes 6291456 | tf_op jit(solution)/shard_map/reduce_scatter | solution.py:67
  273.0 170.5 %reduce-scatter.14.cloned.1.call-start = ((), (), s32[]{:S(2)}) async-start(), calls=%async_computation.21 | async-start | bytes 6291456 | tf_op jit(solution)/shard_map/reduce_scatter | solution.py:68
  280.2 164.3 %copy-start.1 = (bf16[2048,512]{1,0:T(8,128)(2,1)S(1)}, bf16[2048,512]{1,0:T(8,128)(2,1)}, u32[]{:S(2)}) copy-start(bf16[2048,512]{1,0:T(8,128)(2,1)} %param.7) | copy-start | bytes 6291460
Sparse Core Ops, SparseCore 0:
  10.4 106.0 all-gather.2
  131.0 39.7 reduce-scatter.5
  173.3 45.4 reduce-scatter.7
  244.2 28.8 all-gather.4
  275.5 112.8 reduce-scatter.9
  391.4 20.9 reduce-scatter.11
  415.5 18.7 reduce-scatter.13

commit v8 on v6

--- a/solution.py
+++ b/solution.py
@@ -92,7 +92,7 @@
         tm=tm,
         chan=chan,
         chan_near=chan // far,
-        stages=((CHAN + TM + ("dp",), mesh.size),),
+        stages=((("dp",), dp), (("cx",), chan // far), (("zh",), far), (TM, tm)),
     )
     token = P(TM, "dp", CHAN)
     return jax.shard_map(

time: 455 us -> 438 us (0.963)
  local copies, waits for them, and re-layouts: 23.5 us -> 14.3 us
  blocking collectives: 253 us -> 247 us
    dot_general x2 -> x0, local copies, waits for them, and re-layouts: 8.45 us -> none  [on_device(): jnp.einsum('btc,blc->tl', gate, whole_x, preferred_element_type=jnp.float32)]
    all_to_all x3 -> x6, blocking collectives: 93.2 us -> 86.8 us  [gather_a2a(): y = lax.all_to_all(b, axis_name, 0, 0, tiled=True)]
    unnamed x31 -> x32, local copies, waits for them, and re-layouts: 8.19 us -> 9.14 us
    all_to_all x3 -> x6, blocking collectives: 160 us -> 161 us  [scatter_a2a(): lax.all_to_all(p.reshape((size, p.shape[0] // size) + p.shape[1:]), axis_...]
  transfers between devices with their start and end apart: 4 -> 4, of which waited for: 2 -> 2; matrix products, arithmetic and copies ran while one was open for 7% -> 5% of each run, Pallas kernels for 0% -> 0%
where the time goes in v8:
time: 438 us; the launch traced here: 437 us
  blocking collectives  247 us (56%)
  waiting for transfers between devices  109 us (25%)
  matrix products  38.5 us (9%)
  local copies, waits for them, and re-layouts  14.3 us (3%)
  between operations  14 us (3%)
  other arithmetic  13.1 us (3%)
    all_to_all x6, blocking collectives, scatter_a2a(): lax.all_to_all(p.reshape((size, p.shape[0] // size) + p.shape[1:]), axis_...  161 us
    all_gather x1, waiting for transfers between devices, on_device(): pair = lax.all_gather(own, TM, axis=2, tiled=True)  107 us
    all_to_all x6, blocking collectives, gather_a2a(): y = lax.all_to_all(b, axis_name, 0, 0, tiled=True)  86.8 us
    unnamed x32, local copies, waits for them, and re-layouts  9.14 us
  transfers between devices with their start and end apart: 4, of which 2 were waited for; matrix products, arithmetic and copies ran while one was open for 5% of the time, Pallas kernels for 0%

profile of v8, /device:TPU:1, one launch (start us, length us, event | category | flops | bytes accessed | tf_op | source)
XLA Modules:
  0.0 436.8 jit_solution(6076313547695591283)
XLA Ops:
  9.5 107.0 %all-gather.2.cloned.1.call-done = bf16[2,2,512,2048]{3,2,1,0:T(8,128)(2,1)} async-done(((bf16[2,2,32,2048]{3,2,1,0:T(8,128)(2,1)}), bf16[2,2,512,2048]{3,2,1,0:T(8,128)(2,1)}) %all-gather.2.cloned.1.call-update) | async-done | bytes 8388624 | tf_op jit(solution)/shard_map/all_gather | solution.py:44
  116.4 2.7 slice.25
  119.3 2.4 fusion.20
  123.5 6.5 %add_convert_fusion = (bf16[2,512,2048]{2,1,0:T(8,128)(2,1)S(1)}, f32[2,2048,512]{1,2,0:T(8,128)}) fusion(bf16[2,2,512,2048]{3,2,1,0:T(8,128)(2,1)S(1)} %bitcast.104, bf16[512,512]{1,0:T(8,128)(2,1)S(1)} %copy-done.7), kind=kOutput, calls=%fused_computation.12 | convolution fusion | flops 2170552320 | bytes 21495808 | tf_op jit(solution)/shard_map/tl,blc->btc/dot_general | solution.py:47
  130.0 2.3 fusion.17
  133.2 51.6 %all_to_all.60 = f32[4,256,2,512]{3,1,2,0:T(8,128)} all-to-all(f32[4,256,2,512]{3,1,2,0:T(8,128)S(1)} %copy.61), channel_id=1, replica_groups=mesh['zh'=2,'cx'=4,'tz'=4,'ty'=4,'dp'=2] {'cx'}, dimensions={0} | all-to-all | bytes 8388608 | tf_op jit(solution)/shard_map/all_to_all | solution.py:37
  184.9 2.8 reduce_sum.54
  187.7 21.7 %all_to_all.61 = f32[2,128,2,512]{3,1,2,0:T(8,128)S(1)} all-to-all(f32[2,128,2,512]{3,1,2,0:T(8,128)S(1)} %copy.63), channel_id=1, replica_groups=mesh['zh'=2,'cx'=4,'tz'=4,'ty'=4,'dp'=2] {'zh'}, dimensions={0} | all-to-all | bytes 2097152 | tf_op jit(solution)/shard_map/all_to_all | solution.py:37
  211.7 11.7 %all_to_all.62 = bf16[2,128,2,512]{3,1,2,0:T(8,128)(2,1)S(1)} all-to-all(bf16[2,128,2,512]{3,1,2,0:T(8,128)(2,1)S(1)} %broadcast_in_dim.40), channel_id=1, replica_groups=mesh['zh'=2,'cx'=4,'tz'=4,'ty'=4,'dp'=2] {'zh'}, dimensions={0} | all-to-all | bytes 1048576 | tf_op jit(solution)/shard_map/all_to_all | solution.py:32
  223.6 18.1 %all_to_all.63 = bf16[4,256,2,512]{3,1,2,0:T(8,128)(2,1)S(1)} all-to-all(bf16[4,256,2,512]{3,1,2,0:T(8,128)(2,1)S(1)} %broadcast_in_dim.42), channel_id=1, replica_groups=mesh['zh'=2,'cx'=4,'tz'=4,'ty'=4,'dp'=2] {'cx'}, dimensions={0} | all-to-all | bytes 4194304 | tf_op jit(solution)/shard_map/all_to_all | solution.py:32
  241.9 2.4 multiply_add_fusion.1
  246.1 5.5 %fusion.6 = bf16[2,512,2048]{2,1,0:T(8,128)(2,1)S(1)} fusion(f32[2,512,2048]{2,1,0:T(8,128)S(1)} %bitcast.88, f32[2,2048,512]{1,2,0:T(8,128)S(1)} %bitcast.95), kind=kLoop, calls=%fused_computation.8 | loop fusion | flops 39845888 | bytes 20971520 | tf_op jit(solution)/shard_map/convert_element_type | solution.py:71
  253.5 6.0 %bitcast_add_fusion = f32[2,512,2048]{2,1,0:T(8,128)} fusion(f32[2,512,2048]{2,1,0:T(8,128)S(1)} %bitcast.89, bf16[2,512,2048]{2,1,0:T(8,128)(2,1)S(1)} %fusion.6, bf16[512,512]{1,0:T(8,128)(2,1)S(1)} %copy-done.8), kind=kOutput, calls=%fused_computation.9 | convolution fusion | flops 2149580800 | bytes 21495808 | tf_op jit(solution)/shard_map/tl,btc->blc/dot_general | solution.py:72
  261.1 6.5 %fusion.27 = f32[2048,512]{1,0:T(8,128)} fusion(bf16[1024,2048]{1,0:T(8,128)(2,1)} %bitcast.109, bf16[1024,2,512]{2,0,1:T(8,128)(2,1)S(1)} %bitcast.97), kind=kOutput, calls=%fused_computation.30 | convolution fusion | flops 2147483648 | bytes 9437184 | tf_op jit(solution)/shard_map/rc,rh->ch/dot_general | solution.py:61
  267.9 6.5 %fusion.26 = f32[512,2048]{1,0:T(8,128)} fusion(bf16[1024,2048]{1,0:T(8,128)(2,1)} %bitcast.91, bf16[1024,2,512]{2,0,1:T(8,128)(2,1)S(1)} %bitcast.98), kind=kOutput, calls=%fused_computation.28 | convolution fusion | flops 2147483648 | bytes 9437184 | tf_op jit(solution)/shard_map/rh,rc->hc/dot_general | solution.py:62
  274.5 5.8 %fusion.23 = f32[2,256,512]{2,1,0:T(8,128)S(1)} fusion(bf16[2,256,2,2048]{3,1,0,2:T(8,128)(2,1)} %bitcast.93, bf16[2,2,512,2048]{3,2,1,0:T(8,128)(2,1)} %all-gather.2.cloned.1.call-done), kind=kOutput, calls=%fused_computation.26 | convolution fusion | flops 2147483648 | bytes 9437184 | tf_op jit(solution)/shard_map/btc,blc->tl/dot_general | solution.py:75
  280.3 20.9 %all_to_all.64 = f32[2,256,512]{2,1,0:T(8,128)S(1)} all-to-all(f32[2,256,512]{2,1,0:T(8,128)S(1)} %fusion.23), channel_id=1, replica_groups=mesh['zh'=2,'cx'=4,'tz'=4,'ty'=4,'dp'=2] {'dp'}, dimensions={0} | all-to-all | bytes 2097152 | tf_op jit(solution)/shard_map/all_to_all | solution.py:37
  301.3 11.5 %all_to_all.65 = f32[4,64,512]{2,1,0:T(8,128)S(1)} all-to-all(f32[4,64,512]{2,1,0:T(8,128)S(1)} %bitcast.105), channel_id=1, replica_groups=mesh['zh'=2,'cx'=4,'tz'=4,'ty'=4,'dp'=2] {'cx'}, dimensions={0} | all-to-all | bytes 1048576 | tf_op jit(solution)/shard_map/all_to_all | solution.py:37
  312.8 11.3 %all_to_all.66 = f32[2,32,512]{2,1,0:T(8,128)S(1)} all-to-all(f32[2,32,512]{2,1,0:T(8,128)S(1)} %bitcast.107), channel_id=1, replica_groups=mesh['zh'=2,'cx'=4,'tz'=4,'ty'=4,'dp'=2] {'zh'}, dimensions={0} | all-to-all | bytes 262144 | tf_op jit(solution)/shard_map/all_to_all | solution.py:37
  324.2 43.5 %all_to_all.67 = f32[16,2,512]{2,1,0:T(2,128)S(1)} all-to-all(f32[16,2,512]{2,1,0:T(2,128)S(1)} %reshape.63), channel_id=1, replica_groups=mesh['zh'=2,'cx'=4,'tz'=4,'ty'=4,'dp'=2] {'tz','ty'}, dimensions={0} | all-to-all | bytes 131072 | tf_op jit(solution)/shard_map/all_to_all | solution.py:37
  367.8 26.0 %all_to_all.68 = f32[16,2,512]{2,1,0:T(2,128)S(1)} all-to-all(f32[16,2,512]{2,1,0:T(2,128)S(1)} %broadcast_in_dim.43), channel_id=1, replica_groups=mesh['zh'=2,'cx'=4,'tz'=4,'ty'=4,'dp'=2] {'tz','ty'}, dimensions={0} | all-to-all | bytes 131072 | tf_op jit(solution)/shard_map/all_to_all | solution.py:32
  393.8 11.3 %all_to_all.69 = f32[2,32,512]{2,1,0:T(8,128)S(1)} all-to-all(f32[2,32,512]{2,1,0:T(8,128)S(1)} %broadcast_in_dim.45), channel_id=1, replica_groups=mesh['zh'=2,'cx'=4,'tz'=4,'ty'=4,'dp'=2] {'zh'}, dimensions={0} | all-to-all | bytes 262144 | tf_op jit(solution)/shard_map/all_to_all | solution.py:32
  405.2 10.5 %all_to_all.70 = f32[4,64,512]{2,1,0:T(8,128)S(1)} all-to-all(f32[4,64,512]{2,1,0:T(8,128)S(1)} %broadcast_in_dim.47), channel_id=1, replica_groups=mesh['zh'=2,'cx'=4,'tz'=4,'ty'=4,'dp'=2] {'cx'}, dimensions={0} | all-to-all | bytes 1048576 | tf_op jit(solution)/shard_map/all_to_all | solution.py:32
  415.9 9.2 %all_to_all.71 = f32[2,256,512]{2,1,0:T(8,128)S(1)} all-to-all(f32[2,256,512]{2,1,0:T(8,128)S(1)} %broadcast_in_dim.49), channel_id=1, replica_groups=mesh['zh'=2,'cx'=4,'tz'=4,'ty'=4,'dp'=2] {'dp'}, dimensions={0} | all-to-all | bytes 2097152 | tf_op jit(solution)/shard_map/all_to_all | solution.py:32
  (68 shorter events, 18.9 us)
Async XLA Ops:
  7.2 122.8 %copy-start = (bf16[2048,512]{1,0:T(8,128)(2,1)S(1)}, bf16[2048,512]{1,0:T(8,128)(2,1)}, u32[]{:S(2)}) copy-start(bf16[2048,512]{1,0:T(8,128)(2,1)} %param.7) | copy-start | bytes 6291460
  7.2 109.3 %all-gather.2.cloned.1.call-start = ((), (), s32[]{:S(2)}) async-start(), calls=%async_computation.15 | async-start | bytes 8912896 | tf_op jit(solution)/shard_map/all_gather | solution.py:44
  9.4 415.7 %reduce-scatter.4.cloned.1.call-start = ((), (), s32[]{:S(2)}) async-start(), calls=%async_computation.16 | async-start | bytes 8912896 | tf_op jit(solution)/shard_map/reduce_scatter | solution.py:73
  116.4 2.9 copy-start.9
  116.4 5.3 %slice-start.2 = ((s8[8388608]{0:T(1024)(128)(4,1)}), s8[4194304]{0:T(1024)(128)(4,1)S(1)}, s32[]{:S(2)}) async-start(s8[8388608]{0:T(1024)(128)(4,1)} %bitcast.103), calls=%async_computation.21 | async-start | bytes 8388608
  119.1 2.6 copy-start.2
  119.3 4.2 slice-start.3
  119.3 4.2 copy-start.7
  130.0 2.3 copy-start.10
  223.6 18.3 %copy-start.3 = (bf16[1,2,512,2048]{3,2,1,0:T(8,128)(2,1)S(1)}, bf16[1,2,512,2048]{3,2,1,0:T(8,128)(2,1)}, u32[]{:S(2)}) copy-start(bf16[1,2,512,2048]{3,2,1,0:T(8,128)(2,1)} %copy-done.2) | copy-start | bytes 12582916
  241.9 2.5 copy-start.5
  241.9 2.9 slice-start
  241.9 4.2 slice-start.1
  246.1 7.4 %copy-start.8 = (bf16[512,512]{1,0:T(8,128)(2,1)S(1)}, bf16[512,512]{1,0:T(8,128)(2,1)}, u32[]{:S(2)}) copy-start(bf16[512,512]{1,0:T(8,128)(2,1)} %param.9) | copy-start | bytes 1572868
  251.6 1.9 copy-start.4
  259.5 1.6 copy-start.6
  259.5 167.8 %reduce-scatter.6.cloned.1.call-start = ((), (), s32[]{:S(2)}) async-start(), calls=%async_computation.17 | async-start | bytes 6291456 | tf_op jit(solution)/shard_map/reduce_scatter | solution.py:64
  267.6 161.7 %reduce-scatter.8.cloned.1.call-start = ((), (), s32[]{:S(2)}) async-start(), calls=%async_computation.18 | async-start | bytes 6291456 | tf_op jit(solution)/shard_map/reduce_scatter | solution.py:65
  405.2 25.1 %copy-start.1 = (bf16[2048,512]{1,0:T(8,128)(2,1)S(1)}, bf16[2048,512]{1,0:T(8,128)(2,1)}, u32[]{:S(2)}) copy-start(bf16[2048,512]{1,0:T(8,128)(2,1)} %param.7) | copy-start | bytes 6291460
Sparse Core Ops, SparseCore 0:
  10.4 106.0 all-gather.1
  259.6 123.1 reduce-scatter.3
  385.9 21.5 reduce-scatter.5
  410.4 18.7 reduce-scatter.7

commit v9 on v8

--- a/solution.py
+++ b/solution.py
@@ -62,7 +62,7 @@
     wout_part = jnp.einsum("rh,rc->hc", activation, grad_rows, preferred_element_type=jnp.float32)
     grad_w_in, grad_w_out = (
         lax.psum_scatter(win_part, "dp", scatter_dimension=1, tiled=True),
-        lax.psum_scatter(wout_part, "dp", scatter_dimension=0, tiled=True),
+        scatter_a2a(wout_part, "dp", 2),
     )
     share = jnp.einsum("rh,ch->rc", pre_grad, w_in, preferred_element_type=jnp.float32) + grad_rows.astype(
         jnp.float32
@@ -92,7 +92,13 @@
         tm=tm,
         chan=chan,
         chan_near=chan // far,
-        stages=((("dp",), dp), (("cx",), chan // far), (("zh",), far), (TM, tm)),
+        stages=(
+            (("dp",), dp),
+            (("cx",), chan // far),
+            (("zh",), far),
+            (("ty",), tm // near_z),
+            (("tz",), near_z),
+        ),
     )
     token = P(TM, "dp", CHAN)
     return jax.shard_map(

time: 438 us -> 470 us (1.073)
  starting transfers between devices: 0.38 us -> 66.7 us
  blocking collectives: 247 us -> 192 us
  waiting for transfers between devices: 109 us -> 118 us
  local copies, waits for them, and re-layouts: 14.3 us -> 19.6 us
  other arithmetic: 13.1 us -> 17.9 us
    all_to_all x0 -> x4, starting transfers between devices: none -> 66.6 us  [the longest x2 59.1 us: scatter_a2a(): lax.all_to_all(p.reshape((size, p.shape[0] // size) + p.shape[1:]), axis_...]
    all_to_all x6, blocking collectives: 161 us -> 132 us  [scatter_a2a(): lax.all_to_all(p.reshape((size, p.shape[0] // size) + p.shape[1:]), axis_...]
    all_to_all x6 -> x5, blocking collectives: 86.8 us -> 59.4 us  [gather_a2a(): y = lax.all_to_all(b, axis_name, 0, 0, tiled=True)]
    all_to_all x0 -> x4, waiting for transfers between devices: none -> 10.7 us  [the longest x2 7.96 us: scatter_a2a(): lax.all_to_all(p.reshape((size, p.shape[0] // size) + p.shape[1:]), axis_...]
    reduce_sum x6 -> x8, other arithmetic: 3.87 us -> 8.8 us  [scatter_a2a(): return y.sum(0)]
  transfers between devices with their start and end apart: 4 -> 7, of which waited for: 2 -> 4; matrix products, arithmetic and copies ran while one was open for 5% -> 6% of each run, Pallas kernels for 0% -> 0%
where the time goes in v9:
time: 470 us; the launch traced here: 469 us
  blocking collectives  192 us (41%)
  waiting for transfers between devices  118 us (25%)
  starting transfers between devices  66.7 us (14%)
  matrix products  41 us (9%)
  local copies, waits for them, and re-layouts  19.6 us (4%)
  other arithmetic  17.9 us (4%)
  between operations  14 us (3%)
    all_to_all x6, blocking collectives, scatter_a2a(): lax.all_to_all(p.reshape((size, p.shape[0] // size) + p.shape[1:]), axis_...  132 us
    all_gather x1, waiting for transfers between devices, on_device(): pair = lax.all_gather(own, TM, axis=2, tiled=True)  107 us
    all_to_all x5, blocking collectives, gather_a2a(): y = lax.all_to_all(b, axis_name, 0, 0, tiled=True)  59.4 us
    all_to_all x2, starting transfers between devices, scatter_a2a(): lax.all_to_all(p.reshape((size, p.shape[0] // size) + p.shape[1:]), axis_...  59.1 us
  transfers between devices with their start and end apart: 7, of which 4 were waited for; matrix products, arithmetic and copies ran while one was open for 6% of the time, Pallas kernels for 0%

profile of v9, /device:TPU:1, one launch (start us, length us, event | category | flops | bytes accessed | tf_op | source)
XLA Modules:
  0.0 468.8 jit_solution(8502295992846266221)
XLA Ops:
  9.5 107.0 %all-gather.2.cloned.1.call-done = bf16[2,2,512,2048]{3,2,1,0:T(8,128)(2,1)} async-done(((bf16[2,2,32,2048]{3,2,1,0:T(8,128)(2,1)}), bf16[2,2,512,2048]{3,2,1,0:T(8,128)(2,1)}) %all-gather.2.cloned.1.call-update) | async-done | bytes 8388624 | tf_op jit(solution)/shard_map/all_gather | solution.py:44
  123.5 6.5 %add_convert_fusion = (bf16[2,512,2048]{2,1,0:T(8,128)(2,1)S(1)}, f32[2,2048,512]{1,2,0:T(8,128)}) fusion(bf16[2,2,512,2048]{3,2,1,0:T(8,128)(2,1)S(1)} %bitcast.110, bf16[512,512]{1,0:T(8,128)(2,1)S(1)} %copy-done.5), kind=kOutput, calls=%fused_computation.12 | convolution fusion | flops 2170552320 | bytes 21495808 | tf_op jit(solution)/shard_map/tl,blc->btc/dot_general | solution.py:47
  133.2 51.6 %all_to_all.75 = f32[4,256,2,512]{3,1,2,0:T(8,128)} all-to-all(f32[4,256,2,512]{3,1,2,0:T(8,128)S(1)} %copy.65), channel_id=1, replica_groups=mesh['zh'=2,'cx'=4,'tz'=4,'ty'=4,'dp'=2] {'cx'}, dimensions={0} | all-to-all | bytes 8388608 | tf_op jit(solution)/shard_map/all_to_all | solution.py:37
  187.7 21.8 %all_to_all.76 = f32[2,128,2,512]{3,1,2,0:T(8,128)S(1)} all-to-all(f32[2,128,2,512]{3,1,2,0:T(8,128)S(1)} %copy.67), channel_id=1, replica_groups=mesh['zh'=2,'cx'=4,'tz'=4,'ty'=4,'dp'=2] {'zh'}, dimensions={0} | all-to-all | bytes 2097152 | tf_op jit(solution)/shard_map/all_to_all | solution.py:37
  211.9 11.7 %all_to_all.77 = bf16[2,128,2,512]{1,3,2,0:T(8,128)(2,1)S(1)} all-to-all(bf16[2,128,2,512]{1,3,2,0:T(8,128)(2,1)S(1)} %broadcast_in_dim.47), channel_id=1, replica_groups=mesh['zh'=2,'cx'=4,'tz'=4,'ty'=4,'dp'=2] {'zh'}, dimensions={0} | all-to-all | bytes 1048576 | tf_op jit(solution)/shard_map/all_to_all | solution.py:32
  224.2 18.6 %all_to_all.78 = bf16[4,256,2,512]{1,3,2,0:T(8,128)(2,1)} all-to-all(bf16[4,256,2,512]{1,3,2,0:T(8,128)(2,1)S(1)} %broadcast_in_dim.49), channel_id=1, replica_groups=mesh['zh'=2,'cx'=4,'tz'=4,'ty'=4,'dp'=2] {'cx'}, dimensions={0} | all-to-all | bytes 4194304 | tf_op jit(solution)/shard_map/all_to_all | solution.py:32
  242.8 4.1 copy.72
  246.9 5.0 %multiply_add_fusion.1 = f32[1024,2048]{1,0:T(8,128)S(1)} fusion(bf16[1,2,512,2048]{3,2,1,0:T(8,128)(2,1)} %copy-done.4, bf16[2048,512]{1,0:T(8,128)(2,1)S(1)} %copy-done, bf16[1024,2,512]{2,0,1:T(8,128)(2,1)} %bitcast.101), kind=kOutput, calls=%fused_computation.11 | convolution fusion | flops 2153775104 | bytes 15728640 | tf_op jit(solution)/shard_map/rh,ch->rc/dot_general | solution.py:67
  252.0 5.5 %fusion.6 = bf16[2,512,2048]{2,1,0:T(8,128)(2,1)S(1)} fusion(f32[2,512,2048]{2,1,0:T(8,128)S(1)} %bitcast.96, f32[2,2048,512]{1,2,0:T(8,128)S(1)} %bitcast.100), kind=kLoop, calls=%fused_computation.8 | loop fusion | flops 39845888 | bytes 20971520 | tf_op jit(solution)/shard_map/convert_element_type | solution.py:71
  259.5 6.0 %bitcast_add_fusion = f32[2,512,2048]{2,1,0:T(8,128)} fusion(f32[2,512,2048]{2,1,0:T(8,128)S(1)} %bitcast.97, bf16[2,512,2048]{2,1,0:T(8,128)(2,1)S(1)} %fusion.6, bf16[512,512]{1,0:T(8,128)(2,1)S(1)} %copy-done.6), kind=kOutput, calls=%fused_computation.9 | convolution fusion | flops 2149580800 | bytes 21495808 | tf_op jit(solution)/shard_map/tl,btc->blc/dot_general | solution.py:72
  267.0 6.5 %fusion.26 = f32[2048,512]{1,0:T(8,128)} fusion(bf16[1024,2048]{1,0:T(8,128)(2,1)} %bitcast.119, bf16[1024,2,512]{2,0,1:T(8,128)(2,1)S(1)} %bitcast.102), kind=kOutput, calls=%fused_computation.29 | convolution fusion | flops 2147483648 | bytes 9437184 | tf_op jit(solution)/shard_map/rc,rh->ch/dot_general | solution.py:61
  273.6 5.8 %fusion.23 = f32[2,256,512]{2,1,0:T(8,128)S(1)} fusion(bf16[2,256,2,2048]{3,1,0,2:T(8,128)(2,1)} %bitcast.98, bf16[2,2,512,2048]{3,2,1,0:T(8,128)(2,1)} %all-gather.2.cloned.1.call-done), kind=kOutput, calls=%fused_computation.26 | convolution fusion | flops 2147483648 | bytes 9437184 | tf_op jit(solution)/shard_map/btc,blc->tl/dot_general | solution.py:75
  279.4 20.8 %all_to_all.79 = f32[2,256,512]{2,1,0:T(8,128)S(1)} all-to-all(f32[2,256,512]{2,1,0:T(8,128)S(1)} %fusion.23), channel_id=1, replica_groups=mesh['zh'=2,'cx'=4,'tz'=4,'ty'=4,'dp'=2] {'dp'}, dimensions={0} | all-to-all | bytes 2097152 | tf_op jit(solution)/shard_map/all_to_all | solution.py:37
  301.1 12.7 %all_to_all.80 = f32[4,64,512]{2,1,0:T(8,128)S(1)} all-to-all(f32[4,64,512]{2,1,0:T(8,128)} %bitcast.112), channel_id=1, replica_groups=mesh['zh'=2,'cx'=4,'tz'=4,'ty'=4,'dp'=2] {'cx'}, dimensions={0} | all-to-all | bytes 1048576 | tf_op jit(solution)/shard_map/all_to_all | solution.py:37
  313.9 11.4 %all_to_all.81 = f32[2,32,512]{2,1,0:T(8,128)S(1)} all-to-all(f32[2,32,512]{2,1,0:T(8,128)S(1)} %bitcast.115), channel_id=1, replica_groups=mesh['zh'=2,'cx'=4,'tz'=4,'ty'=4,'dp'=2] {'zh'}, dimensions={0} | all-to-all | bytes 262144 | tf_op jit(solution)/shard_map/all_to_all | solution.py:37
  325.3 14.0 %all_to_all.82 = f32[4,8,512]{2,1,0:T(8,128)S(1)} all-to-all(f32[4,8,512]{2,1,0:T(8,128)S(1)} %bitcast.116), channel_id=1, replica_groups=mesh['zh'=2,'cx'=4,'tz'=4,'ty'=4,'dp'=2] {'ty'}, dimensions={0} | all-to-all | bytes 131072 | tf_op jit(solution)/shard_map/all_to_all | solution.py:37
  340.0 51.3 %all-to-all-start.9 = ((f32[4,2,512]{2,1,0:T(2,128)}), f32[4,2,512]{2,1,0:T(2,128)S(1)}, u32[]{:S(2)}, u32[]{:S(2)}) async-start(f32[4,2,512]{2,1,0:T(2,128)} %reshape.70), calls=%async_computation.11 | async-start | bytes 32768 | tf_op jit(solution)/shard_map/all_to_all | solution.py:37
  399.8 6.5 %fusion.36 = f32[2,256,2048]{2,1,0:T(8,128)} fusion(bf16[2,256,1024]{2,1,0:T(8,128)(2,1)S(1)} %bitcast.113, bf16[1024,2048,1]{1,0,2:T(8,128)(2,1)} %bitcast.105), kind=kOutput, calls=%fused_computation.47 | convolution fusion | flops 2147483648 | bytes 9437184 | tf_op jit(solution)/shard_map/rh,rc->hc/dot_general | solution.py:62
  406.3 7.8 %all-to-all-start.4 = ((f32[2,256,2048]{2,1,0:T(8,128)}), f32[2,256,2048]{2,1,0:T(8,128)}, u32[]{:S(2)}, u32[]{:S(2)}) async-start(f32[2,256,2048]{2,1,0:T(8,128)} %fusion.36), calls=%async_computation.6 | async-start | bytes 8388608 | tf_op jit(solution)/shard_map/all_to_all | solution.py:37
  414.1 4.1 all-to-all-done.4
  418.3 7.8 %all_to_all.83 = f32[4,8,512]{2,1,0:T(8,128)S(1)} all-to-all(f32[4,8,512]{2,1,0:T(8,128)S(1)} %broadcast_in_dim.52), channel_id=1, replica_groups=mesh['zh'=2,'cx'=4,'tz'=4,'ty'=4,'dp'=2] {'ty'}, dimensions={0} | all-to-all | bytes 131072 | tf_op jit(solution)/shard_map/all_to_all | solution.py:32
  426.1 12.6 %all_to_all.84 = f32[2,32,512]{2,1,0:T(8,128)S(1)} all-to-all(f32[2,32,512]{2,1,0:T(8,128)S(1)} %broadcast_in_dim.54), channel_id=1, replica_groups=mesh['zh'=2,'cx'=4,'tz'=4,'ty'=4,'dp'=2] {'zh'}, dimensions={0} | all-to-all | bytes 262144 | tf_op jit(solution)/shard_map/all_to_all | solution.py:32
  443.5 4.2 reduce_sum.74
  450.6 8.7 %all_to_all.85 = f32[2,256,512]{2,1,0:T(8,128)S(1)} all-to-all(f32[2,256,512]{2,1,0:T(8,128)S(1)} %broadcast_in_dim.58), channel_id=1, replica_groups=mesh['zh'=2,'cx'=4,'tz'=4,'ty'=4,'dp'=2] {'dp'}, dimensions={0} | all-to-all | bytes 2097152 | tf_op jit(solution)/shard_map/all_to_all | solution.py:32
  (75 shorter events, 42.7 us)
Async XLA Ops:
  7.2 122.8 %copy-start = (bf16[2048,512]{1,0:T(8,128)(2,1)S(1)}, bf16[2048,512]{1,0:T(8,128)(2,1)}, u32[]{:S(2)}) copy-start(bf16[2048,512]{1,0:T(8,128)(2,1)} %param.7) | copy-start | bytes 6291460
  7.2 109.3 %all-gather.2.cloned.1.call-start = ((), (), s32[]{:S(2)}) async-start(), calls=%async_computation.17 | async-start | bytes 8912896 | tf_op jit(solution)/shard_map/all_gather | solution.py:44
  9.4 449.8 %reduce-scatter.3.cloned.1.call-start = ((), (), s32[]{:S(2)}) async-start(), calls=%async_computation.18 | async-start | bytes 8912896 | tf_op jit(solution)/shard_map/reduce_scatter | solution.py:73
  116.4 2.9 copy-start.7
  116.4 5.3 %slice-start.2 = ((s8[8388608]{0:T(1024)(128)(4,1)}), s8[4194304]{0:T(1024)(128)(4,1)S(1)}, s32[]{:S(2)}) async-start(s8[8388608]{0:T(1024)(128)(4,1)} %bitcast.109), calls=%async_computation.22 | async-start | bytes 8388608
  119.1 2.6 copy-start.4
  119.3 4.2 slice-start.3
  119.3 4.2 copy-start.5
  130.0 2.3 copy-start.8
  246.9 5.0 %slice-start = ((s8[8388608]{0:T(1024)(128)(4,1)}), s8[4194304]{0:T(1024)(128)(4,1)S(1)}, s32[]{:S(2)}) async-start(s8[8388608]{0:T(1024)(128)(4,1)} %bitcast.99), calls=%async_computation.20 | async-start | bytes 8388608
  246.9 5.0 %slice-start.1 = ((s8[8388608]{0:T(1024)(128)(4,1)}), s8[4194304]{0:T(1024)(128)(4,1)S(1)}, s32[]{:S(2)}) async-start(s8[8388608]{0:T(1024)(128)(4,1)} %bitcast.99), calls=%async_computation.21 | async-start | bytes 8388608
  252.0 7.5 %copy-start.6 = (bf16[512,512]{1,0:T(8,128)(2,1)S(1)}, bf16[512,512]{1,0:T(8,128)(2,1)}, u32[]{:S(2)}) copy-start(bf16[512,512]{1,0:T(8,128)(2,1)} %param.9) | copy-start | bytes 1572868
  257.5 1.9 copy-start.2
  265.4 1.6 copy-start.3
  265.4 195.8 %reduce-scatter.5.cloned.1.call-start = ((), (), s32[]{:S(2)}) async-start(), calls=%async_computation.19 | async-start | bytes 6291456 | tf_op jit(solution)/shard_map/reduce_scatter | solution.py:64
  340.0 55.8 %all-to-all-start.9 = ((f32[4,2,512]{2,1,0:T(2,128)}), f32[4,2,512]{2,1,0:T(2,128)S(1)}, u32[]{:S(2)}, u32[]{:S(2)}) async-start(f32[4,2,512]{2,1,0:T(2,128)} %reshape.70), calls=%async_computation.11 | async-start | bytes 32768 | tf_op jit(solution)/shard_map/all_to_all | solution.py:37
  396.3 10.0 %all-to-all-start.10 = ((f32[4,2,512]{2,1,0:T(2,128)}), f32[4,2,512]{2,1,0:T(2,128)S(1)}, u32[]{:S(2)}, u32[]{:S(2)}) async-start(f32[4,2,512]{2,1,0:T(2,128)} %broadcast_in_dim.50), calls=%async_computation.12 | async-start | bytes 32768 | tf_op jit(solution)/shard_map/all_to_all | solution.py:32
  406.3 12.0 %all-to-all-start.4 = ((f32[2,256,2048]{2,1,0:T(8,128)}), f32[2,256,2048]{2,1,0:T(8,128)}, u32[]{:S(2)}, u32[]{:S(2)}) async-start(f32[2,256,2048]{2,1,0:T(8,128)} %fusion.36), calls=%async_computation.6 | async-start | bytes 8388608 | tf_op jit(solution)/shard_map/all_to_all | solution.py:37
  439.5 10.9 %all-to-all-start.13 = ((f32[4,64,512]{2,1,0:T(8,128)}), f32[4,64,512]{2,1,0:T(8,128)S(1)}, u32[]{:S(2)}, u32[]{:S(2)}) async-start(f32[4,64,512]{2,1,0:T(8,128)} %broadcast_in_dim.56), calls=%async_computation.15 | async-start | bytes 1048576 | tf_op jit(solution)/shard_map/all_to_all | solution.py:32
  443.5 18.7 %copy-start.1 = (bf16[2048,512]{1,0:T(8,128)(2,1)S(1)}, bf16[2048,512]{1,0:T(8,128)(2,1)}, u32[]{:S(2)}) copy-start(bf16[2048,512]{1,0:T(8,128)(2,1)} %param.7) | copy-start | bytes 6291460
Sparse Core Ops, SparseCore 0:
  10.4 106.0 all-gather.1
  265.6 121.7 reduce-scatter.2
  390.5 22.1 reduce-scatter.4
